TPU v7x, 512 devices: a whole 4x4x16 slice. The times are simulated.
512 devices in a mesh: gx: 8 (over z_lo, core), gy: 16 (over x, z_hi), gz: 4 (over y).
Axes of the slice: x: 4, y: 4, z: 16 (z_hi: 4, z_lo: 4; z = z_hi * 4 + z_lo), core: 2. Of those that a mesh axis runs over, the one named last changes fastest.
Arguments:
- heat_source: float32 [128, 256, 512], P('gx', 'gy', 'gz'), may hold values from -6 to 6
- material: int32 [128, 256, 512], P('gx', 'gy', 'gz'), may hold values from 0 to 2
- conductivity: float32 [3], replicated, may hold values from 0.3 to 3
Outputs:
- temperature: float32 [128, 256, 512], P('gx', 'gy', 'gz')
All inputs are finite; a program needn't handle non-finite values.
Results may differ from a plain program's by a relative error of at most 0.00002.
Values sent between devices are 32-bit elements; how exact they have to be, the bound alone decides.
No kernel may reach another device: no remote copies, remote signals or barrier semaphores. Data moves between devices by JAX's collectives and lax.ppermute only.
A program may use at most 192 MiB of HBM per device.

v0:
```python
import jax
import jax.numpy as jnp
from jax import lax
from jax.sharding import PartitionSpec as P

DEGREE = 3
LEVELS = 3
MATERIALS = 3


LOW = 0.3
HIGH = 2.0


def with_halo(block, sides, width):
    for axis, dim in sides:
        count = lax.axis_size(axis)
        forward = [(i, i + 1) for i in range(count - 1)]
        backward = [(target, source) for source, target in forward]
        low = lax.ppermute(
            lax.slice_in_dim(block, block.shape[dim] - width, None, axis=dim), axis, forward
        )
        high = lax.ppermute(lax.slice_in_dim(block, 0, width, axis=dim), axis, backward)
        block = jnp.concatenate([low, block, high], axis=dim)
    return block


def harmonic(left, right):
    return 2.0 * left * right / (left + right)


def neighbours(padded):
    return (
        padded[2:, 1:-1, 1:-1],
        padded[:-2, 1:-1, 1:-1],
        padded[1:-1, 2:, 1:-1],
        padded[1:-1, :-2, 1:-1],
        padded[1:-1, 1:-1, 2:],
        padded[1:-1, 1:-1, :-2],
    )


def spread_field(field):
    return with_halo(field, (("gx", 0), ("gy", 1), ("gz", 2)), 1)


def spread_cond(cond):
    return with_halo(cond, (("gx", 0), ("gy", 1), ("gz", 2)), 1)


def face_set(cond, extend_cond):
    padded = extend_cond(cond)
    faces = tuple(
        (harmonic(cond, jnp.where(other > 0.0, other, cond)) for other in neighbours(padded))
    )
    diag = faces[0] + faces[1] + faces[2] + faces[3] + faces[4] + faces[5]
    return (faces, diag)


def operate(field, faces, diag, scale, extend_field):
    near = neighbours(extend_field(field))
    total = faces[0] * near[0] + faces[1] * near[1] + faces[2] * near[2]
    total = total + faces[3] * near[3] + faces[4] * near[4] + faces[5] * near[5]
    return scale * (diag * field - total)


def smooth(right, start, faces, diag, scale, extend_field):
    theta = 0.5 * (HIGH + LOW)
    delta = 0.5 * (HIGH - LOW)
    sigma = theta / delta
    rho = 1.0 / sigma
    inverse = 1.0 / (scale * diag)
    if start is None:
        resid = right
        step_dir = inverse * resid / theta
        field = step_dir
    else:
        resid = right - operate(start, faces, diag, scale, extend_field)
        step_dir = inverse * resid / theta
        field = start + step_dir
    for turn in range(DEGREE - 1):
        rho_new = 1.0 / (2.0 * sigma - rho)
        resid = right - operate(field, faces, diag, scale, extend_field)
        step_dir = rho_new * rho * step_dir + 2.0 * rho_new / delta * inverse * resid
        field = field + step_dir
        rho = rho_new
    return field


def restrict(field):
    sx, sy, sz = field.shape
    return field.reshape(sx // 2, 2, sy // 2, 2, sz // 2, 2).mean(axis=(1, 3, 5))


def prolong(field):
    return jnp.repeat(jnp.repeat(jnp.repeat(field, 2, 0), 2, 1), 2, 2)


def cycle(right, cond, level, scale, extend_field, extend_cond):
    faces, diag = face_set(cond, extend_cond)
    if level == LEVELS:
        field = smooth(right, None, faces, diag, scale, extend_field)
        return smooth(right, field, faces, diag, scale, extend_field)
    field = smooth(right, None, faces, diag, scale, extend_field)
    resid = right - operate(field, faces, diag, scale, extend_field)
    error = cycle(
        restrict(resid), restrict(cond), level + 1, scale * 0.25, extend_field, extend_cond
    )
    field = field + prolong(error)
    return smooth(right, field, faces, diag, scale, extend_field)


def local(heat_source, material, conductivity):
    cond = jnp.zeros(heat_source.shape, jnp.float32)
    for which in range(MATERIALS):
        cond = cond + jnp.where(material == which, conductivity[which], jnp.float32(0.0))
    faces, diag = face_set(cond, spread_cond)
    field = smooth(heat_source, None, faces, diag, 1.0, spread_field)
    resid = heat_source - operate(field, faces, diag, 1.0, spread_field)
    coarse_right = restrict(resid)
    coarse_cond = restrict(cond)
    error = cycle(coarse_right, coarse_cond, 1, 0.25, spread_field, spread_cond)
    field = field + prolong(error)
    return smooth(heat_source, field, faces, diag, 1.0, spread_field)


def solution(mesh):
    in_specs = (P("gx", "gy", "gz"), P("gx", "gy", "gz"), P())
    out_specs = P("gx", "gy", "gz")
    return jax.shard_map(local, mesh=mesh, in_specs=in_specs, out_specs=out_specs, check_vma=False)
```

profile of v0, /device:TPU:1, one launch (start us, length us, event | category | flops | bytes accessed | tf_op | source)
XLA Modules:
  0.0 798.6 jit_solution(10578287427865433512)
XLA Ops:
  4.2 4.9 collective-permute-start.1
  9.2 5.1 collective-permute-start
  15.1 7.8 collective-permute-start.3
  24.3 7.7 collective-permute-done.2
  54.1 7.0 collective-permute-start.9
  62.4 7.0 collective-permute-done.8
  86.4 9.7 %reshape.47 = f32[8,2,8,2,64,2]{5,4,3,2,1,0:T(8,128)} reshape(f32[16,16,128]{2,1,0:T(8,128)S(1)} %select_add_fusion) | data formatting | bytes 262144 | tf_op jit(solution)/shard_map/reshape | solution.py:92
  105.5 7.0 collective-permute-done.14
  113.9 4.7 collective-permute-start.17
  120.9 5.1 collective-permute-start.19
  135.3 7.9 collective-permute-start.27
  144.6 6.9 collective-permute-done.26
  162.4 9.7 %reshape.48 = f32[8,2,8,2,64,2]{5,4,3,2,1,0:T(8,128)} reshape(f32[16,16,128]{2,1,0:T(8,128)S(1)} %fusion.48) | data formatting | bytes 262144 | tf_op jit(solution)/shard_map/reshape | solution.py:92
  176.3 6.5 collective-permute-start.31
  187.7 7.1 collective-permute-start.33
  196.1 7.0 collective-permute-done.32
  204.5 4.9 collective-permute-start.35
  220.2 6.1 collective-permute-start.39
  227.6 6.9 collective-permute-done.38
  251.0 4.9 collective-permute-start.45
  257.3 7.9 collective-permute-start.51
  266.5 6.9 collective-permute-done.50
  287.6 7.3 collective-permute-start.55
  305.6 5.0 collective-permute-done.56
  327.0 6.6 collective-permute-start.63
  334.9 7.9 collective-permute-start.69
  358.1 8.0 %collective-permute-start.75 = (f32[6,1,32]{2,1,0:T(1,128)S(1)}, f32[6,1,32]{2,1,0:T(1,128)S(1)}, u32[]{:S(2)}, u32[]{:S(2)}) collective-permute-start(f32[6,1,32]{2,1,0:T(1,128)S(1)} %get-tuple-element.154), channel_id=1, source_target_pairs={{0,4},{4,8},{8,12},{12,16},{16,20},{20,24},{24,28},{28,32},{32,36}... | collective-permute-start | bytes 2312 | tf_op jit(solution)/shard_map/ppermute | solution.py:20
  394.3 7.0 collective-permute-start.81
  402.6 6.9 collective-permute-done.80
  430.7 6.9 collective-permute-done.86
  453.5 5.8 collective-permute-start.93
  460.7 6.9 collective-permute-done.92
  483.5 5.0 collective-permute-start.99
  489.8 6.9 collective-permute-done.98
  512.7 5.1 collective-permute-start.105
  519.1 6.9 collective-permute-done.104
  547.7 6.9 collective-permute-done.110
  570.7 5.9 collective-permute-start.117
  577.9 6.9 collective-permute-done.116
  601.0 5.0 collective-permute-start.123
  607.3 6.9 collective-permute-done.122
  634.7 7.0 collective-permute-done.128
  662.2 7.0 collective-permute-done.134
  689.9 7.0 collective-permute-done.140
  719.6 7.0 collective-permute-done.146
  749.3 7.0 collective-permute-done.152
  757.8 4.7 collective-permute-start.155
  779.2 7.0 collective-permute-done.158
  (456 shorter events, 476.2 us)
Async XLA Ops:
  4.2 10.1 %collective-permute-start.1 = (f32[1,16,128]{2,1,0:T(8,128)S(1)}, f32[1,16,128]{2,1,0:T(8,128)S(1)}, u32[]{:S(2)}, u32[]{:S(2)}) collective-permute-start(f32[1,16,128]{2,1,0:T(8,128)S(1)} %get-tuple-element.90), channel_id=1, source_target_pairs={{0,64},{64,128},{128,192},{192,256},{256,320},{320,384},{384,448},... | collective-permute-start | bytes 24584 | tf_op jit(solution)/shard_map/ppermute | solution.py:20
  15.1 9.1 %collective-permute-start.3 = (f32[18,1,128]{2,1,0:T(1,128)S(1)}, f32[18,1,128]{2,1,0:T(1,128)S(1)}, u32[]{:S(2)}, u32[]{:S(2)}) collective-permute-start(f32[18,1,128]{2,1,0:T(1,128)S(1)} %get-tuple-element.76), channel_id=1, source_target_pairs={{0,4},{4,8},{8,12},{12,16},{16,20},{20,24},{24,28},{28,32},{32,36}... | collective-permute-start | bytes 27656 | tf_op jit(solution)/shard_map/ppermute | solution.py:20
  23.0 9.0 %collective-permute-start.2 = (f32[18,1,128]{2,1,0:T(1,128)S(1)}, f32[18,1,128]{2,1,0:T(1,128)S(1)}, u32[]{:S(2)}, u32[]{:S(2)}) collective-permute-start(f32[18,1,128]{2,1,0:T(1,128)S(1)} %get-tuple-element.77), channel_id=1, source_target_pairs={{4,0},{8,4},{12,8},{16,12},{20,16},{24,20},{28,24},{32,28},{36,32}... | collective-permute-start | bytes 27656 | tf_op jit(solution)/shard_map/ppermute | solution.py:23
  35.3 9.3 %collective-permute-start.4 = (f32[18,18,1]{2,1,0:T(8,128)S(1)}, f32[18,18,1]{2,1,0:T(8,128)S(1)}, u32[]{:S(2)}, u32[]{:S(2)}) collective-permute-start(f32[18,18,1]{2,1,0:T(8,128)S(1)} %get-tuple-element.63), channel_id=1, source_target_pairs={{1,0},{2,1},{3,2},{5,4},{6,5},{7,6},{9,8},{10,9},{11,10},{13,12},{... | collective-permute-start | bytes 3896 | tf_op jit(solution)/shard_map/ppermute | solution.py:23
  54.1 8.3 %collective-permute-start.9 = (f32[18,1,128]{2,1,0:T(1,128)S(1)}, f32[18,1,128]{2,1,0:T(1,128)S(1)}, u32[]{:S(2)}, u32[]{:S(2)}) collective-permute-start(f32[18,1,128]{2,1,0:T(1,128)S(1)} %get-tuple-element.74), channel_id=1, source_target_pairs={{0,4},{4,8},{8,12},{12,16},{16,20},{20,24},{24,28},{28,32},{32,36}... | collective-permute-start | bytes 27656 | tf_op jit(solution)/shard_map/ppermute | solution.py:20
  69.6 9.3 %collective-permute-start.10 = (f32[18,18,1]{2,1,0:T(8,128)S(1)}, f32[18,18,1]{2,1,0:T(8,128)S(1)}, u32[]{:S(2)}, u32[]{:S(2)}) collective-permute-start(f32[18,18,1]{2,1,0:T(8,128)S(1)} %get-tuple-element.60), channel_id=1, source_target_pairs={{1,0},{2,1},{3,2},{5,4},{6,5},{7,6},{9,8},{10,9},{11,10},{13,12},{... | collective-permute-start | bytes 3896 | tf_op jit(solution)/shard_map/ppermute | solution.py:23
  70.9 8.9 %collective-permute-start.11 = (f32[18,18,1]{2,1,0:T(8,128)S(1)}, f32[18,18,1]{2,1,0:T(8,128)S(1)}, u32[]{:S(2)}, u32[]{:S(2)}) collective-permute-start(f32[18,18,1]{2,1,0:T(8,128)S(1)} %get-tuple-element.61), channel_id=1, source_target_pairs={{0,1},{1,2},{2,3},{4,5},{5,6},{6,7},{8,9},{9,10},{10,11},{12,13},{... | collective-permute-start | bytes 3896 | tf_op jit(solution)/shard_map/ppermute | solution.py:20
  81.1 19.0 %collective-permute-start.13 = (f32[1,16,128]{2,1,0:T(8,128)S(1)}, f32[1,16,128]{2,1,0:T(8,128)S(1)}, u32[]{:S(2)}, u32[]{:S(2)}) collective-permute-start(f32[1,16,128]{2,1,0:T(8,128)S(1)} %get-tuple-element.86), channel_id=1, source_target_pairs={{0,64},{64,128},{128,192},{192,256},{256,320},{320,384},{384,448},... | collective-permute-start | bytes 24584 | tf_op jit(solution)/shard_map/ppermute | solution.py:20
  84.3 15.8 %collective-permute-start.12 = (f32[1,16,128]{2,1,0:T(8,128)S(1)}, f32[1,16,128]{2,1,0:T(8,128)S(1)}, u32[]{:S(2)}, u32[]{:S(2)}) collective-permute-start(f32[1,16,128]{2,1,0:T(8,128)S(1)} %get-tuple-element.87), channel_id=1, source_target_pairs={{64,0},{128,64},{192,128},{256,192},{320,256},{384,320},{448,384},... | collective-permute-start | bytes 24584 | tf_op jit(solution)/shard_map/ppermute | solution.py:23
  112.6 13.4 %collective-permute-start.16 = (f32[18,18,1]{2,1,0:T(8,128)S(1)}, f32[18,18,1]{2,1,0:T(8,128)S(1)}, u32[]{:S(2)}, u32[]{:S(2)}) collective-permute-start(f32[18,18,1]{2,1,0:T(8,128)S(1)} %get-tuple-element.58), channel_id=1, source_target_pairs={{1,0},{2,1},{3,2},{5,4},{6,5},{7,6},{9,8},{10,9},{11,10},{13,12},{... | collective-permute-start | bytes 3896 | tf_op jit(solution)/shard_map/ppermute | solution.py:23
  113.9 12.1 %collective-permute-start.17 = (f32[18,18,1]{2,1,0:T(8,128)S(1)}, f32[18,18,1]{2,1,0:T(8,128)S(1)}, u32[]{:S(2)}, u32[]{:S(2)}) collective-permute-start(f32[18,18,1]{2,1,0:T(8,128)S(1)} %get-tuple-element.59), channel_id=1, source_target_pairs={{0,1},{1,2},{2,3},{4,5},{5,6},{6,7},{8,9},{9,10},{10,11},{12,13},{... | collective-permute-start | bytes 3896 | tf_op jit(solution)/shard_map/ppermute | solution.py:20
  118.7 12.2 %collective-permute-start.18 = (f32[1,8,64]{2,1,0:T(8,128)S(1)}, f32[1,8,64]{2,1,0:T(8,128)S(1)}, u32[]{:S(2)}, u32[]{:S(2)}) collective-permute-start(f32[1,8,64]{2,1,0:T(8,128)S(1)} %get-tuple-element.132), channel_id=1, source_target_pairs={{64,0},{128,64},{192,128},{256,192},{320,256},{384,320},{448,384},... | collective-permute-start | bytes 6152 | tf_op jit(solution)/shard_map/ppermute | solution.py:23
  120.9 10.1 %collective-permute-start.19 = (f32[1,8,64]{2,1,0:T(8,128)S(1)}, f32[1,8,64]{2,1,0:T(8,128)S(1)}, u32[]{:S(2)}, u32[]{:S(2)}) collective-permute-start(f32[1,8,64]{2,1,0:T(8,128)S(1)} %get-tuple-element.133), channel_id=1, source_target_pairs={{0,64},{64,128},{128,192},{192,256},{256,320},{320,384},{384,448},... | collective-permute-start | bytes 6152 | tf_op jit(solution)/shard_map/ppermute | solution.py:20
  126.6 8.7 %collective-permute-start.25 = (f32[1,16,128]{2,1,0:T(8,128)S(1)}, f32[1,16,128]{2,1,0:T(8,128)S(1)}, u32[]{:S(2)}, u32[]{:S(2)}) collective-permute-start(f32[1,16,128]{2,1,0:T(8,128)S(1)} %get-tuple-element.84), channel_id=1, source_target_pairs={{0,64},{64,128},{128,192},{192,256},{256,320},{320,384},{384,448},... | collective-permute-start | bytes 24584 | tf_op jit(solution)/shard_map/ppermute | solution.py:20
  131.0 13.5 %collective-permute-start.21 = (f32[10,1,64]{2,1,0:T(1,128)S(1)}, f32[10,1,64]{2,1,0:T(1,128)S(1)}, u32[]{:S(2)}, u32[]{:S(2)}) collective-permute-start(f32[10,1,64]{2,1,0:T(1,128)S(1)} %get-tuple-element.118), channel_id=1, source_target_pairs={{0,4},{4,8},{8,12},{12,16},{16,20},{20,24},{24,28},{28,32},{32,36}... | collective-permute-start | bytes 7688 | tf_op jit(solution)/shard_map/ppermute | solution.py:20
  134.0 10.6 %collective-permute-start.20 = (f32[10,1,64]{2,1,0:T(1,128)S(1)}, f32[10,1,64]{2,1,0:T(1,128)S(1)}, u32[]{:S(2)}, u32[]{:S(2)}) collective-permute-start(f32[10,1,64]{2,1,0:T(1,128)S(1)} %get-tuple-element.119), channel_id=1, source_target_pairs={{4,0},{8,4},{12,8},{16,12},{20,16},{24,20},{28,24},{32,28},{36,32}... | collective-permute-start | bytes 7688 | tf_op jit(solution)/shard_map/ppermute | solution.py:23
  135.3 9.3 %collective-permute-start.27 = (f32[18,1,128]{2,1,0:T(1,128)S(1)}, f32[18,1,128]{2,1,0:T(1,128)S(1)}, u32[]{:S(2)}, u32[]{:S(2)}) collective-permute-start(f32[18,1,128]{2,1,0:T(1,128)S(1)} %get-tuple-element.70), channel_id=1, source_target_pairs={{0,4},{4,8},{8,12},{12,16},{16,20},{20,24},{24,28},{28,32},{32,36}... | collective-permute-start | bytes 27656 | tf_op jit(solution)/shard_map/ppermute | solution.py:20
  151.7 10.3 %collective-permute-start.28 = (f32[18,18,1]{2,1,0:T(8,128)S(1)}, f32[18,18,1]{2,1,0:T(8,128)S(1)}, u32[]{:S(2)}, u32[]{:S(2)}) collective-permute-start(f32[18,18,1]{2,1,0:T(8,128)S(1)} %get-tuple-element.56), channel_id=1, source_target_pairs={{1,0},{2,1},{3,2},{5,4},{6,5},{7,6},{9,8},{10,9},{11,10},{13,12},{... | collective-permute-start | bytes 3896 | tf_op jit(solution)/shard_map/ppermute | solution.py:23
  153.0 9.0 %collective-permute-start.29 = (f32[18,18,1]{2,1,0:T(8,128)S(1)}, f32[18,18,1]{2,1,0:T(8,128)S(1)}, u32[]{:S(2)}, u32[]{:S(2)}) collective-permute-start(f32[18,18,1]{2,1,0:T(8,128)S(1)} %get-tuple-element.57), channel_id=1, source_target_pairs={{0,1},{1,2},{2,3},{4,5},{5,6},{6,7},{8,9},{9,10},{10,11},{12,13},{... | collective-permute-start | bytes 3896 | tf_op jit(solution)/shard_map/ppermute | solution.py:20
  157.4 18.7 %collective-permute-start.23 = (f32[10,10,1]{2,1,0:T(8,128)S(1)}, f32[10,10,1]{2,1,0:T(8,128)S(1)}, u32[]{:S(2)}, u32[]{:S(2)}) collective-permute-start(f32[10,10,1]{2,1,0:T(8,128)S(1)} %get-tuple-element.104), channel_id=1, source_target_pairs={{0,1},{1,2},{2,3},{4,5},{5,6},{6,7},{8,9},{9,10},{10,11},{12,13},{... | collective-permute-start | bytes 1208 | tf_op jit(solution)/shard_map/ppermute | solution.py:20
  160.7 15.4 %collective-permute-start.22 = (f32[10,10,1]{2,1,0:T(8,128)S(1)}, f32[10,10,1]{2,1,0:T(8,128)S(1)}, u32[]{:S(2)}, u32[]{:S(2)}) collective-permute-start(f32[10,10,1]{2,1,0:T(8,128)S(1)} %get-tuple-element.105), channel_id=1, source_target_pairs={{1,0},{2,1},{3,2},{5,4},{6,5},{7,6},{9,8},{10,9},{11,10},{13,12},{... | collective-permute-start | bytes 1208 | tf_op jit(solution)/shard_map/ppermute | solution.py:23
  176.3 8.4 %collective-permute-start.31 = (f32[1,8,64]{2,1,0:T(8,128)S(1)}, f32[1,8,64]{2,1,0:T(8,128)S(1)}, u32[]{:S(2)}, u32[]{:S(2)}) collective-permute-start(f32[1,8,64]{2,1,0:T(8,128)S(1)} %get-tuple-element.130), channel_id=1, source_target_pairs={{0,64},{64,128},{128,192},{192,256},{256,320},{320,384},{384,448},... | collective-permute-start | bytes 6152 | tf_op jit(solution)/shard_map/ppermute | solution.py:20
  187.7 8.4 %collective-permute-start.33 = (f32[10,1,64]{2,1,0:T(1,128)S(1)}, f32[10,1,64]{2,1,0:T(1,128)S(1)}, u32[]{:S(2)}, u32[]{:S(2)}) collective-permute-start(f32[10,1,64]{2,1,0:T(1,128)S(1)} %get-tuple-element.116), channel_id=1, source_target_pairs={{0,4},{4,8},{8,12},{12,16},{16,20},{20,24},{24,28},{28,32},{32,36}... | collective-permute-start | bytes 7688 | tf_op jit(solution)/shard_map/ppermute | solution.py:20
  234.7 11.8 %collective-permute-start.40 = (f32[10,10,1]{2,1,0:T(8,128)S(1)}, f32[10,10,1]{2,1,0:T(8,128)S(1)}, u32[]{:S(2)}, u32[]{:S(2)}) collective-permute-start(f32[10,10,1]{2,1,0:T(8,128)S(1)} %get-tuple-element.100), channel_id=1, source_target_pairs={{1,0},{2,1},{3,2},{5,4},{6,5},{7,6},{9,8},{10,9},{11,10},{13,12},{... | collective-permute-start | bytes 1208 | tf_op jit(solution)/shard_map/ppermute | solution.py:23
  236.0 10.5 %collective-permute-start.41 = (f32[10,10,1]{2,1,0:T(8,128)S(1)}, f32[10,10,1]{2,1,0:T(8,128)S(1)}, u32[]{:S(2)}, u32[]{:S(2)}) collective-permute-start(f32[10,10,1]{2,1,0:T(8,128)S(1)} %get-tuple-element.101), channel_id=1, source_target_pairs={{0,1},{1,2},{2,3},{4,5},{5,6},{6,7},{8,9},{9,10},{10,11},{12,13},{... | collective-permute-start | bytes 1208 | tf_op jit(solution)/shard_map/ppermute | solution.py:20
  240.6 10.4 %collective-permute-start.42 = (f32[1,4,32]{2,1,0:T(4,128)S(1)}, f32[1,4,32]{2,1,0:T(4,128)S(1)}, u32[]{:S(2)}, u32[]{:S(2)}) collective-permute-start(f32[1,4,32]{2,1,0:T(4,128)S(1)} %get-tuple-element.186), channel_id=1, source_target_pairs={{64,0},{128,64},{192,128},{256,192},{320,256},{384,320},{448,384},... | collective-permute-start | bytes 1544 | tf_op jit(solution)/shard_map/ppermute | solution.py:23
  242.6 8.4 %collective-permute-start.43 = (f32[1,4,32]{2,1,0:T(4,128)S(1)}, f32[1,4,32]{2,1,0:T(4,128)S(1)}, u32[]{:S(2)}, u32[]{:S(2)}) collective-permute-start(f32[1,4,32]{2,1,0:T(4,128)S(1)} %get-tuple-element.187), channel_id=1, source_target_pairs={{0,64},{64,128},{128,192},{192,256},{256,320},{320,384},{384,448},... | collective-permute-start | bytes 1544 | tf_op jit(solution)/shard_map/ppermute | solution.py:20
  246.7 10.6 %collective-permute-start.49 = (f32[1,8,64]{2,1,0:T(8,128)S(1)}, f32[1,8,64]{2,1,0:T(8,128)S(1)}, u32[]{:S(2)}, u32[]{:S(2)}) collective-permute-start(f32[1,8,64]{2,1,0:T(8,128)S(1)} %get-tuple-element.126), channel_id=1, source_target_pairs={{0,64},{64,128},{128,192},{192,256},{256,320},{320,384},{384,448},... | collective-permute-start | bytes 6152 | tf_op jit(solution)/shard_map/ppermute | solution.py:20
  251.0 15.5 %collective-permute-start.45 = (f32[6,1,32]{2,1,0:T(1,128)S(1)}, f32[6,1,32]{2,1,0:T(1,128)S(1)}, u32[]{:S(2)}, u32[]{:S(2)}) collective-permute-start(f32[6,1,32]{2,1,0:T(1,128)S(1)} %get-tuple-element.160), channel_id=1, source_target_pairs={{0,4},{4,8},{8,12},{12,16},{16,20},{20,24},{24,28},{28,32},{32,36}... | collective-permute-start | bytes 2312 | tf_op jit(solution)/shard_map/ppermute | solution.py:20
  256.0 10.6 %collective-permute-start.44 = (f32[6,1,32]{2,1,0:T(1,128)S(1)}, f32[6,1,32]{2,1,0:T(1,128)S(1)}, u32[]{:S(2)}, u32[]{:S(2)}) collective-permute-start(f32[6,1,32]{2,1,0:T(1,128)S(1)} %get-tuple-element.161), channel_id=1, source_target_pairs={{4,0},{8,4},{12,8},{16,12},{20,16},{24,20},{28,24},{32,28},{36,32}... | collective-permute-start | bytes 2312 | tf_op jit(solution)/shard_map/ppermute | solution.py:23
  257.3 9.2 %collective-permute-start.51 = (f32[10,1,64]{2,1,0:T(1,128)S(1)}, f32[10,1,64]{2,1,0:T(1,128)S(1)}, u32[]{:S(2)}, u32[]{:S(2)}) collective-permute-start(f32[10,1,64]{2,1,0:T(1,128)S(1)} %get-tuple-element.112), channel_id=1, source_target_pairs={{0,4},{4,8},{8,12},{12,16},{16,20},{20,24},{24,28},{28,32},{32,36}... | collective-permute-start | bytes 7688 | tf_op jit(solution)/shard_map/ppermute | solution.py:20
  273.6 10.8 %collective-permute-start.52 = (f32[10,10,1]{2,1,0:T(8,128)S(1)}, f32[10,10,1]{2,1,0:T(8,128)S(1)}, u32[]{:S(2)}, u32[]{:S(2)}) collective-permute-start(f32[10,10,1]{2,1,0:T(8,128)S(1)} %get-tuple-element.98), channel_id=1, source_target_pairs={{1,0},{2,1},{3,2},{5,4},{6,5},{7,6},{9,8},{10,9},{11,10},{13,12},{... | collective-permute-start | bytes 1208 | tf_op jit(solution)/shard_map/ppermute | solution.py:23
  274.9 9.5 %collective-permute-start.53 = (f32[10,10,1]{2,1,0:T(8,128)S(1)}, f32[10,10,1]{2,1,0:T(8,128)S(1)}, u32[]{:S(2)}, u32[]{:S(2)}) collective-permute-start(f32[10,10,1]{2,1,0:T(8,128)S(1)} %get-tuple-element.99), channel_id=1, source_target_pairs={{0,1},{1,2},{2,3},{4,5},{5,6},{6,7},{8,9},{9,10},{10,11},{12,13},{... | collective-permute-start | bytes 1208 | tf_op jit(solution)/shard_map/ppermute | solution.py:20
  287.6 9.3 %collective-permute-start.55 = (f32[1,4,32]{2,1,0:T(4,128)S(1)}, f32[1,4,32]{2,1,0:T(4,128)S(1)}, u32[]{:S(2)}, u32[]{:S(2)}) collective-permute-start(f32[1,4,32]{2,1,0:T(4,128)S(1)} %get-tuple-element.184), channel_id=1, source_target_pairs={{0,64},{64,128},{128,192},{192,256},{256,320},{320,384},{384,448},... | collective-permute-start | bytes 1544 | tf_op jit(solution)/shard_map/ppermute | solution.py:20
  303.7 20.8 %collective-permute-start.66 = (f32[1,2,16]{2,1,0:T(2,128)S(1)}, f32[1,2,16]{2,1,0:T(2,128)S(1)}, u32[]{:S(2)}, u32[]{:S(2)}) collective-permute-start(f32[1,2,16]{2,1,0:T(2,128)S(1)} %get-tuple-element.210), channel_id=1, source_target_pairs={{64,0},{128,64},{192,128},{256,192},{320,256},{384,320},{448,384},... | collective-permute-start | bytes 392 | tf_op jit(solution)/shard_map/ppermute | solution.py:23
  310.7 9.2 %collective-permute-start.58 = (f32[6,6,1]{2,1,0:T(8,128)S(1)}, f32[6,6,1]{2,1,0:T(8,128)S(1)}, u32[]{:S(2)}, u32[]{:S(2)}) collective-permute-start(f32[6,6,1]{2,1,0:T(8,128)S(1)} %get-tuple-element.144), channel_id=1, source_target_pairs={{1,0},{2,1},{3,2},{5,4},{6,5},{7,6},{9,8},{10,9},{11,10},{13,12},{... | collective-permute-start | bytes 440 | tf_op jit(solution)/shard_map/ppermute | solution.py:23
  327.0 15.9 %collective-permute-start.63 = (f32[6,1,32]{2,1,0:T(1,128)S(1)}, f32[6,1,32]{2,1,0:T(1,128)S(1)}, u32[]{:S(2)}, u32[]{:S(2)}) collective-permute-start(f32[6,1,32]{2,1,0:T(1,128)S(1)} %get-tuple-element.156), channel_id=1, source_target_pairs={{0,4},{4,8},{8,12},{12,16},{16,20},{20,24},{24,28},{28,32},{32,36}... | collective-permute-start | bytes 2312 | tf_op jit(solution)/shard_map/ppermute | solution.py:20
  333.6 9.2 %collective-permute-start.62 = (f32[6,1,32]{2,1,0:T(1,128)S(1)}, f32[6,1,32]{2,1,0:T(1,128)S(1)}, u32[]{:S(2)}, u32[]{:S(2)}) collective-permute-start(f32[6,1,32]{2,1,0:T(1,128)S(1)} %get-tuple-element.157), channel_id=1, source_target_pairs={{4,0},{8,4},{12,8},{16,12},{20,16},{24,20},{28,24},{32,28},{36,32}... | collective-permute-start | bytes 2312 | tf_op jit(solution)/shard_map/ppermute | solution.py:23
  334.9 20.2 %collective-permute-start.69 = (f32[4,1,16]{2,1,0:T(1,128)S(1)}, f32[4,1,16]{2,1,0:T(1,128)S(1)}, u32[]{:S(2)}, u32[]{:S(2)}) collective-permute-start(f32[4,1,16]{2,1,0:T(1,128)S(1)} %get-tuple-element.198), channel_id=1, source_target_pairs={{0,4},{4,8},{8,12},{12,16},{16,20},{20,24},{24,28},{28,32},{32,36}... | collective-permute-start | bytes 776 | tf_op jit(solution)/shard_map/ppermute | solution.py:20
  358.1 13.0 %collective-permute-start.75 = (f32[6,1,32]{2,1,0:T(1,128)S(1)}, f32[6,1,32]{2,1,0:T(1,128)S(1)}, u32[]{:S(2)}, u32[]{:S(2)}) collective-permute-start(f32[6,1,32]{2,1,0:T(1,128)S(1)} %get-tuple-element.154), channel_id=1, source_target_pairs={{0,4},{4,8},{8,12},{12,16},{16,20},{20,24},{24,28},{28,32},{32,36}... | collective-permute-start | bytes 2312 | tf_op jit(solution)/shard_map/ppermute | solution.py:20
  367.5 14.2 %collective-permute-start.71 = (f32[4,4,1]{2,1,0:T(4,128)S(1)}, f32[4,4,1]{2,1,0:T(4,128)S(1)}, u32[]{:S(2)}, u32[]{:S(2)}) collective-permute-start(f32[4,4,1]{2,1,0:T(4,128)S(1)} %get-tuple-element.178), channel_id=1, source_target_pairs={{0,1},{1,2},{2,3},{4,5},{5,6},{6,7},{8,9},{9,10},{10,11},{12,13},{... | collective-permute-start | bytes 200 | tf_op jit(solution)/shard_map/ppermute | solution.py:20
  726.8 9.4 %collective-permute-start.148 = (f32[18,18,1]{2,1,0:T(8,128)S(1)}, f32[18,18,1]{2,1,0:T(8,128)S(1)}, u32[]{:S(2)}, u32[]{:S(2)}) collective-permute-start(f32[18,18,1]{2,1,0:T(8,128)S(1)} %get-tuple-element.54), channel_id=1, source_target_pairs={{1,0},{2,1},{3,2},{5,4},{6,5},{7,6},{9,8},{10,9},{11,10},{13,12},{... | collective-permute-start | bytes 3896 | tf_op jit(solution)/shard_map/ppermute | solution.py:23
  728.1 9.9 %collective-permute-start.149 = (f32[18,18,1]{2,1,0:T(8,128)S(1)}, f32[18,18,1]{2,1,0:T(8,128)S(1)}, u32[]{:S(2)}, u32[]{:S(2)}) collective-permute-start(f32[18,18,1]{2,1,0:T(8,128)S(1)} %get-tuple-element.55), channel_id=1, source_target_pairs={{0,1},{1,2},{2,3},{4,5},{5,6},{6,7},{8,9},{9,10},{10,11},{12,13},{... | collective-permute-start | bytes 3896 | tf_op jit(solution)/shard_map/ppermute | solution.py:20
  756.5 9.9 %collective-permute-start.154 = (f32[18,18,1]{2,1,0:T(8,128)S(1)}, f32[18,18,1]{2,1,0:T(8,128)S(1)}, u32[]{:S(2)}, u32[]{:S(2)}) collective-permute-start(f32[18,18,1]{2,1,0:T(8,128)S(1)} %get-tuple-element.52), channel_id=1, source_target_pairs={{1,0},{2,1},{3,2},{5,4},{6,5},{7,6},{9,8},{10,9},{11,10},{13,12},{... | collective-permute-start | bytes 3896 | tf_op jit(solution)/shard_map/ppermute | solution.py:23
  757.8 9.8 %collective-permute-start.155 = (f32[18,18,1]{2,1,0:T(8,128)S(1)}, f32[18,18,1]{2,1,0:T(8,128)S(1)}, u32[]{:S(2)}, u32[]{:S(2)}) collective-permute-start(f32[18,18,1]{2,1,0:T(8,128)S(1)} %get-tuple-element.53), channel_id=1, source_target_pairs={{0,1},{1,2},{2,3},{4,5},{5,6},{6,7},{8,9},{9,10},{10,11},{12,13},{... | collective-permute-start | bytes 3896 | tf_op jit(solution)/shard_map/ppermute | solution.py:20
  777.8 8.3 %collective-permute-start.158 = (f32[18,1,128]{2,1,0:T(1,128)S(1)}, f32[18,1,128]{2,1,0:T(1,128)S(1)}, u32[]{:S(2)}, u32[]{:S(2)}) collective-permute-start(f32[18,1,128]{2,1,0:T(1,128)S(1)} %get-tuple-element.65), channel_id=1, source_target_pairs={{4,0},{8,4},{12,8},{16,12},{20,16},{24,20},{28,24},{32,28},{36,32}... | collective-permute-start | bytes 27656 | tf_op jit(solution)/shard_map/ppermute | solution.py:23
  786.3 9.6 %collective-permute-start.160 = (f32[18,18,1]{2,1,0:T(8,128)S(1)}, f32[18,18,1]{2,1,0:T(8,128)S(1)}, u32[]{:S(2)}, u32[]{:S(2)}) collective-permute-start(f32[18,18,1]{2,1,0:T(8,128)S(1)} %get-tuple-element.50), channel_id=1, source_target_pairs={{1,0},{2,1},{3,2},{5,4},{6,5},{7,6},{9,8},{10,9},{11,10},{13,12},{... | collective-permute-start | bytes 3896 | tf_op jit(solution)/shard_map/ppermute | solution.py:23
  787.6 9.9 %collective-permute-start.161 = (f32[18,18,1]{2,1,0:T(8,128)S(1)}, f32[18,18,1]{2,1,0:T(8,128)S(1)}, u32[]{:S(2)}, u32[]{:S(2)}) collective-permute-start(f32[18,18,1]{2,1,0:T(8,128)S(1)} %get-tuple-element.51), channel_id=1, source_target_pairs={{0,1},{1,2},{2,3},{4,5},{5,6},{6,7},{8,9},{9,10},{10,11},{12,13},{... | collective-permute-start | bytes 3896 | tf_op jit(solution)/shard_map/ppermute | solution.py:20
  (115 other events, 749.5 us)
where the time goes:
time: 804 us; the launch traced here: 799 us
  starting transfers between devices  487 us (61%)
  waiting for transfers between devices  262 us (33%)
  local copies, waits for them, and re-layouts  27 us (3%)
  other arithmetic  19.6 us (2%)
    ppermute x81, starting transfers between devices, with_halo(): lax.ppermute(lax.slice_in_dim(block, block.shape[dim] - width, None, axis...  361 us
    ppermute x81, waiting for transfers between devices, with_halo(): lax.ppermute(lax.slice_in_dim(block, 0, width, axis=dim), axis, backward)  240 us
    ppermute x81, starting transfers between devices, with_halo(): lax.ppermute(lax.slice_in_dim(block, 0, width, axis=dim), axis, backward)  126 us
    ppermute x81, waiting for transfers between devices, with_halo(): lax.ppermute(lax.slice_in_dim(block, block.shape[dim] - width, None, axis...  22.4 us
    reshape x4, local copies, waits for them, and re-layouts, restrict(): field.reshape(sx // 2, 2, sy // 2, 2, sz // 2, 2).mean(axis=(1, 3, 5))  20.6 us
  transfers between devices with their start and end apart: 162, of which 73 were waited for; matrix products, arithmetic and copies ran while one was open for 4% of the time, Pallas kernels for 0%

commit v1 on v0

v1 whole, which is shorter than its diff:
```python
import jax
import jax.numpy as jnp
from jax import lax
from jax.sharding import PartitionSpec as P

DEGREE = 3
LEVELS = 3
MATERIALS = 3

LOW = 0.3
HIGH = 2.0

AXES = ("gx", "gy", "gz")
HALO0 = 6
HALO1 = 8


def exchange(block, width):
    for k, axis in enumerate(AXES):
        dim = block.ndim - 3 + k
        count = lax.axis_size(axis)
        forward = [(i, i + 1) for i in range(count - 1)]
        backward = [(i + 1, i) for i in range(count - 1)]
        size = block.shape[dim]
        low = lax.ppermute(lax.slice_in_dim(block, size - width, size, axis=dim), axis, forward)
        high = lax.ppermute(lax.slice_in_dim(block, 0, width, axis=dim), axis, backward)
        block = jnp.concatenate([low, block, high], axis=dim)
    return block


def inside_mask(block_shape, width):
    parts = []
    for k, axis in enumerate(AXES):
        n = block_shape[k]
        total = n * lax.axis_size(axis)
        coord = lax.axis_index(axis) * n - width + jnp.arange(n + 2 * width)
        parts.append((coord >= 0) & (coord < total))
    return parts[0][:, None, None] & parts[1][None, :, None] & parts[2][None, None, :]


def harmonic(left, right):
    return 2.0 * left * right / (left + right)


def neighbours(padded):
    return (
        padded[2:, 1:-1, 1:-1],
        padded[:-2, 1:-1, 1:-1],
        padded[1:-1, 2:, 1:-1],
        padded[1:-1, :-2, 1:-1],
        padded[1:-1, 1:-1, 2:],
        padded[1:-1, 1:-1, :-2],
    )


def face_set_zero_outside(cond):
    padded = jnp.pad(cond, 1)
    faces = tuple(harmonic(cond, jnp.where(other > 0.0, other, cond)) for other in neighbours(padded))
    diag = faces[0] + faces[1] + faces[2] + faces[3] + faces[4] + faces[5]
    return faces, diag


def face_set_global(cond):
    padded = jnp.pad(cond, 1, mode="edge")
    faces = tuple(harmonic(cond, other) for other in neighbours(padded))
    diag = faces[0] + faces[1] + faces[2] + faces[3] + faces[4] + faces[5]
    return faces, diag


def operate(field, faces, diag, scale):
    near = neighbours(jnp.pad(field, 1))
    total = faces[0] * near[0] + faces[1] * near[1] + faces[2] * near[2]
    total = total + faces[3] * near[3] + faces[4] * near[4] + faces[5] * near[5]
    return scale * (diag * field - total)


def smooth(right, start, faces, diag, scale, mask=None):
    def keep(value):
        return value if mask is None else jnp.where(mask, value, 0.0)

    theta = 0.5 * (HIGH + LOW)
    delta = 0.5 * (HIGH - LOW)
    sigma = theta / delta
    rho = 1.0 / sigma
    inverse = 1.0 / (scale * diag)
    if start is None:
        resid = right
        step_dir = inverse * resid / theta
        field = keep(step_dir)
    else:
        resid = right - operate(start, faces, diag, scale)
        step_dir = inverse * resid / theta
        field = keep(start + step_dir)
    for turn in range(DEGREE - 1):
        rho_new = 1.0 / (2.0 * sigma - rho)
        resid = right - operate(field, faces, diag, scale)
        step_dir = rho_new * rho * step_dir + 2.0 * rho_new / delta * inverse * resid
        field = keep(field + step_dir)
        rho = rho_new
    return field


def restrict(field):
    field = field[0::2] + field[1::2]
    field = field[:, 0::2] + field[:, 1::2]
    field = field[:, :, 0::2] + field[:, :, 1::2]
    return field / 8.0


def prolong(field):
    return jnp.repeat(jnp.repeat(jnp.repeat(field, 2, 0), 2, 1), 2, 2)


def centre(field, width):
    return field[width:-width, width:-width, width:-width]


def cycle_global(right, cond, level, scale):
    faces, diag = face_set_global(cond)
    if level == LEVELS:
        field = smooth(right, None, faces, diag, scale)
        return smooth(right, field, faces, diag, scale)
    field = smooth(right, None, faces, diag, scale)
    resid = right - operate(field, faces, diag, scale)
    error = cycle_global(restrict(resid), restrict(cond), level + 1, scale * 0.25)
    field = field + prolong(error)
    return smooth(right, field, faces, diag, scale)


def gather_global(block):
    sizes = [lax.axis_size(axis) for axis in AXES]
    c, bx, by, bz = block.shape
    every = lax.all_gather(block, AXES, axis=0, tiled=False)
    every = every.reshape(sizes[0], sizes[1], sizes[2], c, bx, by, bz)
    every = every.transpose(3, 0, 4, 1, 5, 2, 6)
    return every.reshape(c, sizes[0] * bx, sizes[1] * by, sizes[2] * bz)


def local(heat_source, material, conductivity):
    cond0 = jnp.zeros(heat_source.shape, jnp.float32)
    for which in range(MATERIALS):
        cond0 = cond0 + jnp.where(material == which, conductivity[which], jnp.float32(0.0))
    cond1 = restrict(cond0)
    cond2 = restrict(cond1)
    block0, block1 = heat_source.shape, cond1.shape

    ext0 = exchange(jnp.stack([cond0, heat_source]), HALO0)
    cond0e, right0e = ext0[0], ext0[1]
    mask0 = inside_mask(block0, HALO0)
    faces0, diag0 = face_set_zero_outside(cond0e)
    field0 = smooth(right0e, None, faces0, diag0, 1.0, mask0)
    resid0 = centre(right0e - operate(field0, faces0, diag0, 1.0), HALO0)

    cond1e = exchange(cond1, HALO1)
    faces1, diag1 = face_set_zero_outside(cond1e)
    mask1 = inside_mask(block1, HALO1)
    right1e = exchange(restrict(resid0), HALO1)
    field1 = smooth(right1e, None, faces1, diag1, 0.25, mask1)
    resid1 = centre(right1e - operate(field1, faces1, diag1, 0.25), HALO1)

    whole = gather_global(jnp.stack([cond2, restrict(resid1)]))
    error2 = cycle_global(whole[1], whole[0], 2, 0.0625)

    reach = HALO1 // 2
    padded2 = jnp.pad(error2, reach)
    block2 = cond2.shape
    starts = [lax.axis_index(axis) * n for axis, n in zip(AXES, block2)]
    sizes = [n + 2 * reach for n in block2]
    error2e = lax.dynamic_slice(padded2, starts, sizes)
    field1 = jnp.where(mask1, field1 + prolong(error2e), 0.0)
    field1 = smooth(right1e, field1, faces1, diag1, 0.25, mask1)

    cut = HALO1 - HALO0 // 2
    error1e = field1[cut:-cut, cut:-cut, cut:-cut]
    field0 = jnp.where(mask0, field0 + prolong(error1e), 0.0)
    field0 = smooth(right0e, field0, faces0, diag0, 1.0, mask0)
    return centre(field0, HALO0)


def solution(mesh):
    in_specs = (P("gx", "gy", "gz"), P("gx", "gy", "gz"), P())
    out_specs = P("gx", "gy", "gz")
    return jax.shard_map(local, mesh=mesh, in_specs=in_specs, out_specs=out_specs, check_vma=False)
```

time: 804 us -> 1710 us (2.13)
  waiting for transfers between devices: 262 us -> 1440 us
  starting transfers between devices: 487 us -> 63.9 us
  local copies, waits for them, and re-layouts: 27 us -> 103 us
  other arithmetic: 19.6 us -> 75.4 us
    all_gather x0 -> x1, waiting for transfers between devices: none -> 1410 us  [gather_global(): every = lax.all_gather(block, AXES, axis=0, tiled=False)]
    ppermute x162 -> x18, starting transfers between devices: 487 us -> 63.9 us  [the longest x9 46 us: exchange(): lax.ppermute(lax.slice_in_dim(block, size - width, size, axis=dim), axis,...]
    ppermute x162 -> x18, waiting for transfers between devices: 262 us -> 36 us  [the longest x9 31.1 us: exchange(): lax.ppermute(lax.slice_in_dim(block, 0, width, axis=dim), axis, backward)]
    slice x60 -> x35, local copies, waits for them, and re-layouts: 2.49 us -> 55.9 us  [the longest x12 32.8 us: restrict(): field = field[:, :, 0::2] + field[:, :, 1::2]]
    add x24 -> x28, other arithmetic: 8.07 us -> 33.4 us  [the longest x8 17 us: smooth(): field = keep(field + step_dir)]
  transfers between devices with their start and end apart: 162 -> 19, of which waited for: 73 -> 9; matrix products, arithmetic and copies ran while one was open for 4% -> 1% of each run, Pallas kernels for 0% -> 0%
where the time goes in v1:
time: 1710 us; the launch traced here: 1700 us
  waiting for transfers between devices  1440 us (84%)
  local copies, waits for them, and re-layouts  103 us (6%)
  other arithmetic  75.4 us (4%)
  starting transfers between devices  63.9 us (4%)
    all_gather x1, waiting for transfers between devices, gather_global(): every = lax.all_gather(block, AXES, axis=0, tiled=False)  1410 us
    ppermute x9, starting transfers between devices, exchange(): lax.ppermute(lax.slice_in_dim(block, size - width, size, axis=dim), axis,...  46 us
  transfers between devices with their start and end apart: 19, of which 9 were waited for; matrix products, arithmetic and copies ran while one was open for 1% of the time, Pallas kernels for 0%

profile of v1, /device:TPU:1, one launch (start us, length us, event | category | flops | bytes accessed | tf_op | source)
XLA Modules:
  0.0 1699.5 jit_solution(18156088084440265846)
XLA Ops:
  8.0 2.9 select_add_fusion
  12.1 4.9 collective-permute-start.6
  17.1 5.1 collective-permute-start.7
  22.2 2.9 fusion.339
  25.9 1.9 collective-permute-start
  27.8 2.4 collective-permute-start.1
  34.0 7.3 collective-permute-start.2
  43.4 8.5 collective-permute-start.8
  53.3 14.8 collective-permute-done.3
  69.0 3.2 collective-permute-start.4
  75.0 3.9 collective-permute-done.5
  81.5 2.6 broadcast_multiply_fusion.1
  91.3 1.9 collective-permute-start.12
  93.3 2.4 collective-permute-start.13
  95.8 3.2 collective-permute-start.10
  100.4 11.3 collective-permute-start.14
  115.1 6.9 collective-permute-done.15
  122.2 3.7 collective-permute-start.16
  128.6 2.4 collective-permute-done.16
  131.1 3.8 collective-permute-done.17
  139.6 1406.3 %all-gather.3.cloned.1.call-done = f32[1024,4,4,32]{3,2,1,0:T(4,128)} async-done(((f32[2,4,4,32]{3,2,1,0:T(4,128)}), f32[1024,4,4,32]{3,2,1,0:T(4,128)}) %all-gather.3.cloned.1.call-update) | async-done | bytes 2097168 | tf_op jit(solution)/shard_map/all_gather | solution.py:133
  1545.9 12.1 copy.246
  1557.9 9.6 fusion.329
  1567.5 3.9 squeeze.26
  1573.5 3.7 squeeze.27
  1577.2 5.2 broadcast_multiply_fusion
  1582.4 3.3 fusion.127
  1585.7 4.2 fusion.27
  1589.9 3.0 fusion.41
  1593.8 2.5 slice.872
  1596.2 2.5 slice.873
  1600.5 7.3 slice.874
  1607.8 7.8 slice.875
  1616.4 2.5 slice.848
  1618.9 2.5 slice.849
  1623.1 7.3 slice.850
  1630.4 7.4 slice.851
  1643.8 3.2 copy.236
  1647.0 2.8 broadcast_in_dim.71
  1649.8 3.7 copy.237
  1655.3 3.3 multiply_add_fusion
  1658.6 3.3 fusion.126
  1662.0 4.2 fusion.89
  1674.9 2.7 reshape.150
  1677.6 3.7 copy.242
  1683.6 3.1 and_select_fusion.1
  1686.8 2.3 fusion.128
  1690.3 2.2 fusion.305
  (223 shorter events, 63.2 us)
Async XLA Ops:
  6.5 27.2 %copy-start.35 = (f32[16,16,128]{2,1,0:T(8,128)S(1)}, f32[16,16,128]{2,1,0:T(8,128)}, u32[]{:S(2)}) copy-start(f32[16,16,128]{2,1,0:T(8,128)} %param.3) | copy-start | bytes 393220
  6.5 1539.3 %all-gather.3.cloned.1.call-start = ((), (), s32[]{:S(2)}) async-start(), calls=%async_computation | async-start | bytes 8404992 | tf_op jit(solution)/shard_map/all_gather | solution.py:133
  12.1 31.3 %collective-permute-start.6 = (f32[8,8,64]{2,1,0:T(8,128)S(1)}, f32[8,8,64]{2,1,0:T(8,128)S(1)}, u32[]{:S(2)}, u32[]{:S(2)}) collective-permute-start(f32[8,8,64]{2,1,0:T(8,128)S(1)} %add_multiply_fusion.2), channel_id=1, source_target_pairs={{0,64},{64,128},{128,192},{192,256},{256,320},{320,384},{384,448},... | collective-permute-start | bytes 49160 | tf_op jit(solution)/shard_map/ppermute | solution.py:25
  17.1 26.3 %collective-permute-start.7 = (f32[8,8,64]{2,1,0:T(8,128)S(1)}, f32[8,8,64]{2,1,0:T(8,128)S(1)}, u32[]{:S(2)}, u32[]{:S(2)}) collective-permute-start(f32[8,8,64]{2,1,0:T(8,128)S(1)} %add_multiply_fusion.2), channel_id=1, source_target_pairs={{64,0},{128,64},{192,128},{256,192},{320,256},{384,320},{448,384},... | collective-permute-start | bytes 49160 | tf_op jit(solution)/shard_map/ppermute | solution.py:26
  25.9 6.1 collective-permute-start
  27.8 5.9 collective-permute-start.1
  34.0 19.2 %collective-permute-start.2 = (f32[2,28,6,128]{3,0,2,1:T(2,128)S(1)}, f32[2,28,6,128]{3,0,2,1:T(2,128)S(1)}, u32[]{:S(2)}, u32[]{:S(2)}) collective-permute-start(f32[2,28,6,128]{3,0,2,1:T(2,128)S(1)} %copy.243), channel_id=1, source_target_pairs={{0,4},{4,8},{8,12},{12,16},{16,20},{20,24},{24,28},{28,32},{32,36}... | collective-permute-start | bytes 516104 | tf_op jit(solution)/shard_map/ppermute | solution.py:25
  41.5 26.6 %collective-permute-start.3 = (f32[2,28,6,128]{3,0,2,1:T(2,128)S(1)}, f32[2,28,6,128]{3,0,2,1:T(2,128)S(1)}, u32[]{:S(2)}, u32[]{:S(2)}) collective-permute-start(f32[2,28,6,128]{3,0,2,1:T(2,128)S(1)} %copy.244), channel_id=1, source_target_pairs={{4,0},{8,4},{12,8},{16,12},{20,16},{24,20},{28,24},{32,28},{36,32}... | collective-permute-start | bytes 516104 | tf_op jit(solution)/shard_map/ppermute | solution.py:26
  43.4 30.6 %collective-permute-start.8 = (f32[24,8,64]{2,1,0:T(8,128)S(1)}, f32[24,8,64]{2,1,0:T(8,128)S(1)}, u32[]{:S(2)}, u32[]{:S(2)}) collective-permute-start(f32[24,8,64]{2,1,0:T(8,128)S(1)} %pad_maximum_fusion.47), channel_id=1, source_target_pairs={{0,4},{4,8},{8,12},{12,16},{16,20},{20,24},{24,28},{28,32},{32,36}... | collective-permute-start | bytes 147464 | tf_op jit(solution)/shard_map/ppermute | solution.py:25
  51.9 22.1 %collective-permute-start.9 = (f32[24,8,64]{2,1,0:T(8,128)S(1)}, f32[24,8,64]{2,1,0:T(8,128)S(1)}, u32[]{:S(2)}, u32[]{:S(2)}) collective-permute-start(f32[24,8,64]{2,1,0:T(8,128)S(1)} %pad_maximum_fusion.47), channel_id=1, source_target_pairs={{4,0},{8,4},{12,8},{16,12},{20,16},{24,20},{28,24},{32,28},{36,32}... | collective-permute-start | bytes 147464 | tf_op jit(solution)/shard_map/ppermute | solution.py:26
  69.0 5.5 collective-permute-start.4
  72.7 6.3 collective-permute-start.5
  81.4 5.1 copy-start.8
  81.5 8.0 copy-start.36
  84.2 4.1 copy-start.2
  84.2 4.1 copy-start.4
  84.2 4.1 copy-start.6
  84.2 5.4 copy-start.10
  84.2 5.4 copy-start.12
  84.2 5.4 copy-start.14
  84.2 5.4 copy-start.16
  91.3 9.0 collective-permute-start.12
  93.3 7.1 collective-permute-start.13
  95.8 17.2 %collective-permute-start.10 = (f32[24,24,8]{2,1,0:T(8,128)S(1)}, f32[24,24,8]{2,1,0:T(8,128)S(1)}, u32[]{:S(2)}, u32[]{:S(2)}) collective-permute-start(f32[24,24,8]{2,1,0:T(8,128)S(1)} %get-tuple-element.83), channel_id=1, source_target_pairs={{0,1},{1,2},{2,3},{4,5},{5,6},{6,7},{8,9},{9,10},{10,11},{12,13},{... | collective-permute-start | bytes 55304 | tf_op jit(solution)/shard_map/ppermute | solution.py:25
  99.1 13.9 collective-permute-start.11
  100.4 14.7 collective-permute-start.14
  111.7 10.3 collective-permute-start.15
  122.0 12.9 copy-start.42
  122.2 8.9 collective-permute-start.16
  125.9 9.1 collective-permute-start.17
  128.6 7.1 copy-start.28
  128.6 7.6 copy-start.18
  128.6 7.6 copy-start.20
  128.6 7.6 copy-start.22
  128.6 7.9 copy-start.24
  128.6 7.9 copy-start.26
  1582.4 7.5 copy-start
  1666.4 3.4 copy-start.43
  1667.5 3.5 copy-start.19
  1667.5 3.5 copy-start.21
  1667.5 3.5 copy-start.23
  1667.5 3.5 copy-start.25
  1667.5 3.6 copy-start.27
  1667.5 3.6 copy-start.29
  1667.5 3.6 copy-start.33
  1677.6 3.7 copy-start.40
  1677.6 5.5 copy-start.9
  1677.6 5.5 copy-start.11
  (15 other events, 30.4 us)
Sparse Core Ops, SparseCore 0:
  138.0 1407.7 all-gather.2

commit v2 on v1

--- a/solution.py
+++ b/solution.py
@@ -60,13 +60,6 @@
     return faces, diag
 
 
-def face_set_global(cond):
-    padded = jnp.pad(cond, 1, mode="edge")
-    faces = tuple(harmonic(cond, other) for other in neighbours(padded))
-    diag = faces[0] + faces[1] + faces[2] + faces[3] + faces[4] + faces[5]
-    return faces, diag
-
-
 def operate(field, faces, diag, scale):
     near = neighbours(jnp.pad(field, 1))
     total = faces[0] * near[0] + faces[1] * near[1] + faces[2] * near[2]
@@ -115,25 +108,71 @@
     return field[width:-width, width:-width, width:-width]
 
 
-def cycle_global(right, cond, level, scale):
-    faces, diag = face_set_global(cond)
+def exchange_faces(block):
+    padded = jnp.pad(block, 1)
+    inner = [slice(1, -1)] * 3
+    for k, axis in enumerate(AXES):
+        count = lax.axis_size(axis)
+        forward = [(i, i + 1) for i in range(count - 1)]
+        backward = [(i + 1, i) for i in range(count - 1)]
+        size = block.shape[k]
+        low = lax.ppermute(lax.slice_in_dim(block, size - 1, size, axis=k), axis, forward)
+        high = lax.ppermute(lax.slice_in_dim(block, 0, 1, axis=k), axis, backward)
+        at_low = list(inner)
+        at_low[k] = slice(0, 1)
+        at_high = list(inner)
+        at_high[k] = slice(size + 1, size + 2)
+        padded = padded.at[tuple(at_low)].set(low).at[tuple(at_high)].set(high)
+    return padded
+
+
+def face_set_faces(cond):
+    padded = exchange_faces(cond)
+    faces = tuple(harmonic(cond, jnp.where(other > 0.0, other, cond)) for other in neighbours(padded))
+    diag = faces[0] + faces[1] + faces[2] + faces[3] + faces[4] + faces[5]
+    return faces, diag
+
+
+def operate_faces(field, faces, diag, scale):
+    near = neighbours(exchange_faces(field))
+    total = faces[0] * near[0] + faces[1] * near[1] + faces[2] * near[2]
+    total = total + faces[3] * near[3] + faces[4] * near[4] + faces[5] * near[5]
+    return scale * (diag * field - total)
+
+
+def smooth_faces(right, start, faces, diag, scale):
+    theta = 0.5 * (HIGH + LOW)
+    delta = 0.5 * (HIGH - LOW)
+    sigma = theta / delta
+    rho = 1.0 / sigma
+    inverse = 1.0 / (scale * diag)
+    if start is None:
+        resid = right
+        step_dir = inverse * resid / theta
+        field = step_dir
+    else:
+        resid = right - operate_faces(start, faces, diag, scale)
+        step_dir = inverse * resid / theta
+        field = start + step_dir
+    for turn in range(DEGREE - 1):
+        rho_new = 1.0 / (2.0 * sigma - rho)
+        resid = right - operate_faces(field, faces, diag, scale)
+        step_dir = rho_new * rho * step_dir + 2.0 * rho_new / delta * inverse * resid
+        field = field + step_dir
+        rho = rho_new
+    return field
+
+
+def cycle_faces(right, cond, level, scale):
+    faces, diag = face_set_faces(cond)
     if level == LEVELS:
-        field = smooth(right, None, faces, diag, scale)
-        return smooth(right, field, faces, diag, scale)
-    field = smooth(right, None, faces, diag, scale)
-    resid = right - operate(field, faces, diag, scale)
-    error = cycle_global(restrict(resid), restrict(cond), level + 1, scale * 0.25)
+        field = smooth_faces(right, None, faces, diag, scale)
+        return smooth_faces(right, field, faces, diag, scale)
+    field = smooth_faces(right, None, faces, diag, scale)
+    resid = right - operate_faces(field, faces, diag, scale)
+    error = cycle_faces(restrict(resid), restrict(cond), level + 1, scale * 0.25)
     field = field + prolong(error)
-    return smooth(right, field, faces, diag, scale)
-
-
-def gather_global(block):
-    sizes = [lax.axis_size(axis) for axis in AXES]
-    c, bx, by, bz = block.shape
-    every = lax.all_gather(block, AXES, axis=0, tiled=False)
-    every = every.reshape(sizes[0], sizes[1], sizes[2], c, bx, by, bz)
-    every = every.transpose(3, 0, 4, 1, 5, 2, 6)
-    return every.reshape(c, sizes[0] * bx, sizes[1] * by, sizes[2] * bz)
+    return smooth_faces(right, field, faces, diag, scale)
 
 
 def local(heat_source, material, conductivity):
@@ -158,15 +197,10 @@
     field1 = smooth(right1e, None, faces1, diag1, 0.25, mask1)
     resid1 = centre(right1e - operate(field1, faces1, diag1, 0.25), HALO1)
 
-    whole = gather_global(jnp.stack([cond2, restrict(resid1)]))
-    error2 = cycle_global(whole[1], whole[0], 2, 0.0625)
+    error2 = cycle_faces(restrict(resid1), cond2, 2, 0.0625)
 
     reach = HALO1 // 2
-    padded2 = jnp.pad(error2, reach)
-    block2 = cond2.shape
-    starts = [lax.axis_index(axis) * n for axis, n in zip(AXES, block2)]
-    sizes = [n + 2 * reach for n in block2]
-    error2e = lax.dynamic_slice(padded2, starts, sizes)
+    error2e = jnp.pad(exchange(error2, 3), reach - 3)
     field1 = jnp.where(mask1, field1 + prolong(error2e), 0.0)
     field1 = smooth(right1e, field1, faces1, diag1, 0.25, mask1)
 

time: 1710 us -> 542 us (0.32)
  the two profiles are of different devices: /device:TPU:1 before, /device:TPU:5 now
where the time goes in v2:
time: 542 us; the launch traced here: 533 us
  starting transfers between devices  375 us (69%)
  local copies, waits for them, and re-layouts  72 us (13%)
  other arithmetic  41.9 us (8%)
  waiting for transfers between devices  41.4 us (8%)
    ppermute x39, starting transfers between devices, exchange_faces(): lax.ppermute(lax.slice_in_dim(block, size - 1, size, axis=k), axis, forward)  142 us
    ppermute x39, starting transfers between devices, exchange_faces(): high = lax.ppermute(lax.slice_in_dim(block, 0, 1, axis=k), axis, backward)  140 us
    ppermute x12, starting transfers between devices, exchange(): lax.ppermute(lax.slice_in_dim(block, size - width, size, axis=dim), axis,...  49.8 us
    ppermute x12, starting transfers between devices, exchange(): lax.ppermute(lax.slice_in_dim(block, 0, width, axis=dim), axis, backward)  43 us
    scatter x78, local copies, waits for them, and re-layouts, exchange_faces(): padded = padded.at[tuple(at_low)].set(low).at[tuple(at_high)].set(high)  38.1 us
    ppermute x12, waiting for transfers between devices, exchange(): lax.ppermute(lax.slice_in_dim(block, 0, width, axis=dim), axis, backward)  20.5 us
    ppermute x39, waiting for transfers between devices, exchange_faces(): high = lax.ppermute(lax.slice_in_dim(block, 0, 1, axis=k), axis, backward)  19.4 us
    reshape x8, local copies, waits for them, and re-layouts, prolong(): return jnp.repeat(jnp.repeat(jnp.repeat(field, 2, 0), 2, 1), 2, 2)  14.2 us
  transfers between devices with their start and end apart: 102, of which 22 were waited for; matrix products, arithmetic and copies ran while one was open for 9% of the time, Pallas kernels for 0%

profile of v2, /device:TPU:5, one launch (start us, length us, event | category | flops | bytes accessed | tf_op | source)
XLA Modules:
  0.0 533.2 jit_solution(5749595388057932673)
XLA Ops:
  5.0 4.1 collective-permute-start
  15.1 3.6 collective-permute-start.6
  25.3 3.4 collective-permute-start.36
  34.0 3.3 collective-permute-done.41
  40.2 8.8 %collective-permute-start.38 = (f32[2,1,16]{2,1,0:T(1,128)S(1)}, f32[2,1,16]{2,1,0:T(1,128)S(1)}, u32[]{:S(2)}, u32[]{:S(2)}) collective-permute-start(f32[2,1,16]{2,1,0:T(1,128)S(1)} %get-tuple-element.1105), channel_id=1, source_target_pairs={{0,4},{4,8},{8,12},{12,16},{16,20},{20,24},{24,28},{28,32},{32,36}... | collective-permute-start | bytes 392 | tf_op jit(solution)/shard_map/ppermute | solution.py:119
  49.0 4.7 collective-permute-start.39
  58.0 7.1 %collective-permute-start.20 = (f32[4,1,32]{2,1,0:T(1,128)S(1)}, f32[4,1,32]{2,1,0:T(1,128)S(1)}, u32[]{:S(2)}, u32[]{:S(2)}) collective-permute-start(f32[4,1,32]{2,1,0:T(1,128)S(1)} %get-tuple-element.1067), channel_id=1, source_target_pairs={{0,4},{4,8},{8,12},{12,16},{16,20},{20,24},{24,28},{28,32},{32,36}... | collective-permute-start | bytes 1544 | tf_op jit(solution)/shard_map/ppermute | solution.py:119
  65.1 4.0 collective-permute-start.2
  69.2 6.1 %collective-permute-start.3 = (f32[2,28,6,128]{3,0,2,1:T(2,128)S(1)}, f32[2,28,6,128]{3,0,2,1:T(2,128)S(1)}, u32[]{:S(2)}, u32[]{:S(2)}) collective-permute-start(f32[2,28,6,128]{3,0,2,1:T(2,128)S(1)} %copy.235), channel_id=1, source_target_pairs={{4,0},{8,4},{12,8},{16,12},{20,16},{24,20},{28,24},{32,28},{36,32}... | collective-permute-start | bytes 516104 | tf_op jit(solution)/shard_map/ppermute | solution.py:26
  82.2 4.5 collective-permute-done.21
  86.8 3.6 collective-permute-start.22
  99.9 7.4 %collective-permute-start.9 = (f32[24,8,64]{2,1,0:T(8,128)}, f32[24,8,64]{2,1,0:T(8,128)}, u32[]{:S(2)}, u32[]{:S(2)}) collective-permute-start(f32[24,8,64]{2,1,0:T(8,128)} %pad_maximum_fusion.9), channel_id=1, source_target_pairs={{4,0},{8,4},{12,8},{16,12},{20,16},{24,20},{28,24},{32,28},{36,32}... | collective-permute-start | bytes 147464 | tf_op jit(solution)/shard_map/ppermute | solution.py:26
  109.1 3.4 collective-permute-start.4
  115.9 3.3 collective-permute-done.5
  131.4 12.4 %collective-permute-start.12 = (f32[8,8,64]{2,1,0:T(8,128)S(1)}, f32[8,8,64]{2,1,0:T(8,128)S(1)}, u32[]{:S(2)}, u32[]{:S(2)}) collective-permute-start(f32[8,8,64]{2,1,0:T(8,128)S(1)} %add_multiply_fusion), channel_id=1, source_target_pairs={{0,64},{64,128},{128,192},{192,256},{256,320},{320,384},{384,448},... | collective-permute-start | bytes 49160 | tf_op jit(solution)/shard_map/ppermute | solution.py:25
  145.9 3.2 collective-permute-start.10
  152.3 8.2 %collective-permute-start.15 = (f32[24,8,64]{2,1,0:T(8,128)S(1)}, f32[24,8,64]{2,1,0:T(8,128)S(1)}, u32[]{:S(2)}, u32[]{:S(2)}) collective-permute-start(f32[24,8,64]{2,1,0:T(8,128)S(1)} %pad_maximum_fusion.10), channel_id=1, source_target_pairs={{4,0},{8,4},{12,8},{16,12},{20,16},{24,20},{28,24},{32,28},{36,32}... | collective-permute-start | bytes 147464 | tf_op jit(solution)/shard_map/ppermute | solution.py:26
  161.7 6.2 %collective-permute-done.15 = f32[24,8,64]{2,1,0:T(8,128)S(1)} collective-permute-done((f32[24,8,64]{2,1,0:T(8,128)S(1)}, f32[24,8,64]{2,1,0:T(8,128)S(1)}, u32[]{:S(2)}, u32[]{:S(2)}) %collective-permute-start.15) | collective-permute-done | bytes 49184 | tf_op jit(solution)/shard_map/ppermute | solution.py:26
  168.1 4.0 collective-permute-start.16
  175.8 3.8 collective-permute-done.17
  182.2 7.9 %collective-permute-start.24 = (f32[1,4,32]{2,1,0:T(4,128)S(1)}, f32[1,4,32]{2,1,0:T(4,128)S(1)}, u32[]{:S(2)}, u32[]{:S(2)}) collective-permute-start(f32[1,4,32]{2,1,0:T(4,128)S(1)} %get-tuple-element.1063), channel_id=1, source_target_pairs={{0,64},{64,128},{128,192},{192,256},{256,320},{320,384},{384,448},... | collective-permute-start | bytes 1544 | tf_op jit(solution)/shard_map/ppermute | solution.py:119
  194.0 8.2 %collective-permute-start.27 = (f32[4,1,32]{2,1,0:T(1,128)S(1)}, f32[4,1,32]{2,1,0:T(1,128)S(1)}, u32[]{:S(2)}, u32[]{:S(2)}) collective-permute-start(f32[4,1,32]{2,1,0:T(1,128)S(1)} %get-tuple-element.1060), channel_id=1, source_target_pairs={{4,0},{8,4},{12,8},{16,12},{20,16},{24,20},{28,24},{32,28},{36,32}... | collective-permute-start | bytes 1544 | tf_op jit(solution)/shard_map/ppermute | solution.py:120
  209.4 5.6 %collective-permute-start.30 = (f32[1,4,32]{2,1,0:T(4,128)S(1)}, f32[1,4,32]{2,1,0:T(4,128)S(1)}, u32[]{:S(2)}, u32[]{:S(2)}) collective-permute-start(f32[1,4,32]{2,1,0:T(4,128)S(1)} %get-tuple-element.1057), channel_id=1, source_target_pairs={{0,64},{64,128},{128,192},{192,256},{256,320},{320,384},{384,448},... | collective-permute-start | bytes 1544 | tf_op jit(solution)/shard_map/ppermute | solution.py:119
  218.9 8.2 %collective-permute-start.33 = (f32[4,1,32]{2,1,0:T(1,128)S(1)}, f32[4,1,32]{2,1,0:T(1,128)S(1)}, u32[]{:S(2)}, u32[]{:S(2)}) collective-permute-start(f32[4,1,32]{2,1,0:T(1,128)S(1)} %get-tuple-element.1054), channel_id=1, source_target_pairs={{4,0},{8,4},{12,8},{16,12},{20,16},{24,20},{28,24},{32,28},{36,32}... | collective-permute-start | bytes 1544 | tf_op jit(solution)/shard_map/ppermute | solution.py:120
  235.5 5.6 %collective-permute-start.42 = (f32[1,4,32]{2,1,0:T(4,128)S(1)}, f32[1,4,32]{2,1,0:T(4,128)S(1)}, u32[]{:S(2)}, u32[]{:S(2)}) collective-permute-start(f32[1,4,32]{2,1,0:T(4,128)S(1)} %get-tuple-element.1051), channel_id=1, source_target_pairs={{0,64},{64,128},{128,192},{192,256},{256,320},{320,384},{384,448},... | collective-permute-start | bytes 1544 | tf_op jit(solution)/shard_map/ppermute | solution.py:119
  245.0 8.2 %collective-permute-start.45 = (f32[4,1,32]{2,1,0:T(1,128)S(1)}, f32[4,1,32]{2,1,0:T(1,128)S(1)}, u32[]{:S(2)}, u32[]{:S(2)}) collective-permute-start(f32[4,1,32]{2,1,0:T(1,128)S(1)} %get-tuple-element.1048), channel_id=1, source_target_pairs={{4,0},{8,4},{12,8},{16,12},{20,16},{24,20},{28,24},{32,28},{36,32}... | collective-permute-start | bytes 1544 | tf_op jit(solution)/shard_map/ppermute | solution.py:120
  261.8 5.6 %collective-permute-start.48 = (f32[1,2,16]{2,1,0:T(2,128)S(1)}, f32[1,2,16]{2,1,0:T(2,128)S(1)}, u32[]{:S(2)}, u32[]{:S(2)}) collective-permute-start(f32[1,2,16]{2,1,0:T(2,128)S(1)} %get-tuple-element.1101), channel_id=1, source_target_pairs={{0,64},{64,128},{128,192},{192,256},{256,320},{320,384},{384,448},... | collective-permute-start | bytes 392 | tf_op jit(solution)/shard_map/ppermute | solution.py:119
  271.3 8.2 %collective-permute-start.51 = (f32[2,1,16]{2,1,0:T(1,128)S(1)}, f32[2,1,16]{2,1,0:T(1,128)S(1)}, u32[]{:S(2)}, u32[]{:S(2)}) collective-permute-start(f32[2,1,16]{2,1,0:T(1,128)S(1)} %get-tuple-element.1098), channel_id=1, source_target_pairs={{4,0},{8,4},{12,8},{16,12},{20,16},{24,20},{28,24},{32,28},{36,32}... | collective-permute-start | bytes 392 | tf_op jit(solution)/shard_map/ppermute | solution.py:120
  287.3 5.6 %collective-permute-start.54 = (f32[1,2,16]{2,1,0:T(2,128)S(1)}, f32[1,2,16]{2,1,0:T(2,128)S(1)}, u32[]{:S(2)}, u32[]{:S(2)}) collective-permute-start(f32[1,2,16]{2,1,0:T(2,128)S(1)} %get-tuple-element.1095), channel_id=1, source_target_pairs={{0,64},{64,128},{128,192},{192,256},{256,320},{320,384},{384,448},... | collective-permute-start | bytes 392 | tf_op jit(solution)/shard_map/ppermute | solution.py:119
  296.8 8.2 %collective-permute-start.57 = (f32[2,1,16]{2,1,0:T(1,128)S(1)}, f32[2,1,16]{2,1,0:T(1,128)S(1)}, u32[]{:S(2)}, u32[]{:S(2)}) collective-permute-start(f32[2,1,16]{2,1,0:T(1,128)S(1)} %get-tuple-element.1092), channel_id=1, source_target_pairs={{4,0},{8,4},{12,8},{16,12},{20,16},{24,20},{28,24},{32,28},{36,32}... | collective-permute-start | bytes 392 | tf_op jit(solution)/shard_map/ppermute | solution.py:120
  312.3 5.6 %collective-permute-start.60 = (f32[1,2,16]{2,1,0:T(2,128)S(1)}, f32[1,2,16]{2,1,0:T(2,128)S(1)}, u32[]{:S(2)}, u32[]{:S(2)}) collective-permute-start(f32[1,2,16]{2,1,0:T(2,128)S(1)} %get-tuple-element.1089), channel_id=1, source_target_pairs={{0,64},{64,128},{128,192},{192,256},{256,320},{320,384},{384,448},... | collective-permute-start | bytes 392 | tf_op jit(solution)/shard_map/ppermute | solution.py:119
  321.8 8.2 %collective-permute-start.63 = (f32[2,1,16]{2,1,0:T(1,128)S(1)}, f32[2,1,16]{2,1,0:T(1,128)S(1)}, u32[]{:S(2)}, u32[]{:S(2)}) collective-permute-start(f32[2,1,16]{2,1,0:T(1,128)S(1)} %get-tuple-element.1086), channel_id=1, source_target_pairs={{4,0},{8,4},{12,8},{16,12},{20,16},{24,20},{28,24},{32,28},{36,32}... | collective-permute-start | bytes 392 | tf_op jit(solution)/shard_map/ppermute | solution.py:120
  337.2 5.6 %collective-permute-start.66 = (f32[1,2,16]{2,1,0:T(2,128)S(1)}, f32[1,2,16]{2,1,0:T(2,128)S(1)}, u32[]{:S(2)}, u32[]{:S(2)}) collective-permute-start(f32[1,2,16]{2,1,0:T(2,128)S(1)} %get-tuple-element.1083), channel_id=1, source_target_pairs={{0,64},{64,128},{128,192},{192,256},{256,320},{320,384},{384,448},... | collective-permute-start | bytes 392 | tf_op jit(solution)/shard_map/ppermute | solution.py:119
  346.7 8.2 %collective-permute-start.69 = (f32[2,1,16]{2,1,0:T(1,128)S(1)}, f32[2,1,16]{2,1,0:T(1,128)S(1)}, u32[]{:S(2)}, u32[]{:S(2)}) collective-permute-start(f32[2,1,16]{2,1,0:T(1,128)S(1)} %get-tuple-element.1080), channel_id=1, source_target_pairs={{4,0},{8,4},{12,8},{16,12},{20,16},{24,20},{28,24},{32,28},{36,32}... | collective-permute-start | bytes 392 | tf_op jit(solution)/shard_map/ppermute | solution.py:120
  362.2 5.6 %collective-permute-start.72 = (f32[1,2,16]{2,1,0:T(2,128)S(1)}, f32[1,2,16]{2,1,0:T(2,128)S(1)}, u32[]{:S(2)}, u32[]{:S(2)}) collective-permute-start(f32[1,2,16]{2,1,0:T(2,128)S(1)} %get-tuple-element.1077), channel_id=1, source_target_pairs={{0,64},{64,128},{128,192},{192,256},{256,320},{320,384},{384,448},... | collective-permute-start | bytes 392 | tf_op jit(solution)/shard_map/ppermute | solution.py:119
  371.7 8.2 %collective-permute-start.75 = (f32[2,1,16]{2,1,0:T(1,128)S(1)}, f32[2,1,16]{2,1,0:T(1,128)S(1)}, u32[]{:S(2)}, u32[]{:S(2)}) collective-permute-start(f32[2,1,16]{2,1,0:T(1,128)S(1)} %get-tuple-element.1074), channel_id=1, source_target_pairs={{4,0},{8,4},{12,8},{16,12},{20,16},{24,20},{28,24},{32,28},{36,32}... | collective-permute-start | bytes 392 | tf_op jit(solution)/shard_map/ppermute | solution.py:120
  387.7 5.6 %collective-permute-start.78 = (f32[1,4,32]{2,1,0:T(4,128)S(1)}, f32[1,4,32]{2,1,0:T(4,128)S(1)}, u32[]{:S(2)}, u32[]{:S(2)}) collective-permute-start(f32[1,4,32]{2,1,0:T(4,128)S(1)} %get-tuple-element.1045), channel_id=1, source_target_pairs={{0,64},{64,128},{128,192},{192,256},{256,320},{320,384},{384,448},... | collective-permute-start | bytes 1544 | tf_op jit(solution)/shard_map/ppermute | solution.py:119
  397.3 8.2 %collective-permute-start.81 = (f32[4,1,32]{2,1,0:T(1,128)S(1)}, f32[4,1,32]{2,1,0:T(1,128)S(1)}, u32[]{:S(2)}, u32[]{:S(2)}) collective-permute-start(f32[4,1,32]{2,1,0:T(1,128)S(1)} %get-tuple-element.1042), channel_id=1, source_target_pairs={{4,0},{8,4},{12,8},{16,12},{20,16},{24,20},{28,24},{32,28},{36,32}... | collective-permute-start | bytes 1544 | tf_op jit(solution)/shard_map/ppermute | solution.py:120
  413.0 5.6 %collective-permute-start.84 = (f32[1,4,32]{2,1,0:T(4,128)S(1)}, f32[1,4,32]{2,1,0:T(4,128)S(1)}, u32[]{:S(2)}, u32[]{:S(2)}) collective-permute-start(f32[1,4,32]{2,1,0:T(4,128)S(1)} %get-tuple-element.1039), channel_id=1, source_target_pairs={{0,64},{64,128},{128,192},{192,256},{256,320},{320,384},{384,448},... | collective-permute-start | bytes 1544 | tf_op jit(solution)/shard_map/ppermute | solution.py:119
  422.6 8.2 %collective-permute-start.87 = (f32[4,1,32]{2,1,0:T(1,128)S(1)}, f32[4,1,32]{2,1,0:T(1,128)S(1)}, u32[]{:S(2)}, u32[]{:S(2)}) collective-permute-start(f32[4,1,32]{2,1,0:T(1,128)S(1)} %get-tuple-element.1036), channel_id=1, source_target_pairs={{4,0},{8,4},{12,8},{16,12},{20,16},{24,20},{28,24},{32,28},{36,32}... | collective-permute-start | bytes 1544 | tf_op jit(solution)/shard_map/ppermute | solution.py:120
  438.9 5.6 %collective-permute-start.90 = (f32[1,4,32]{2,1,0:T(4,128)S(1)}, f32[1,4,32]{2,1,0:T(4,128)S(1)}, u32[]{:S(2)}, u32[]{:S(2)}) collective-permute-start(f32[1,4,32]{2,1,0:T(4,128)S(1)} %get-tuple-element.1033), channel_id=1, source_target_pairs={{0,64},{64,128},{128,192},{192,256},{256,320},{320,384},{384,448},... | collective-permute-start | bytes 1544 | tf_op jit(solution)/shard_map/ppermute | solution.py:119
  448.5 8.2 %collective-permute-start.93 = (f32[4,1,32]{2,1,0:T(1,128)S(1)}, f32[4,1,32]{2,1,0:T(1,128)S(1)}, u32[]{:S(2)}, u32[]{:S(2)}) collective-permute-start(f32[4,1,32]{2,1,0:T(1,128)S(1)} %get-tuple-element.1030), channel_id=1, source_target_pairs={{4,0},{8,4},{12,8},{16,12},{20,16},{24,20},{28,24},{32,28},{36,32}... | collective-permute-start | bytes 1544 | tf_op jit(solution)/shard_map/ppermute | solution.py:120
  464.7 5.6 %collective-permute-start.96 = (f32[3,4,32]{2,1,0:T(4,128)S(1)}, f32[3,4,32]{2,1,0:T(4,128)S(1)}, u32[]{:S(2)}, u32[]{:S(2)}) collective-permute-start(f32[3,4,32]{2,1,0:T(4,128)S(1)} %get-tuple-element.1026), channel_id=1, source_target_pairs={{0,64},{64,128},{128,192},{192,256},{256,320},{320,384},{384,448},... | collective-permute-start | bytes 4616 | tf_op jit(solution)/shard_map/ppermute | solution.py:25
  477.2 8.2 %collective-permute-start.99 = (f32[10,3,32]{2,1,0:T(4,128)S(1)}, f32[10,3,32]{2,1,0:T(4,128)S(1)}, u32[]{:S(2)}, u32[]{:S(2)}) collective-permute-start(f32[10,3,32]{2,1,0:T(4,128)S(1)} %get-tuple-element.1025), channel_id=1, source_target_pairs={{4,0},{8,4},{12,8},{16,12},{20,16},{24,20},{28,24},{32,28},{36,32}... | collective-permute-start | bytes 11528 | tf_op jit(solution)/shard_map/ppermute | solution.py:26
  491.5 4.1 collective-permute-done.101
  511.7 3.2 broadcast_in_dim.77
  514.9 3.6 reshape.2589
  518.5 3.6 copy.233
  (509 shorter events, 242.5 us)
Async XLA Ops:
  5.0 20.3 %collective-permute-start = (f32[2,6,16,128]{3,2,1,0:T(8,128)S(1)}, f32[2,6,16,128]{3,2,1,0:T(8,128)S(1)}, u32[]{:S(2)}, u32[]{:S(2)}) collective-permute-start(f32[2,6,16,128]{3,2,1,0:T(8,128)S(1)} %get-tuple-element.1020), channel_id=1, source_target_pairs={{0,64},{64,128},{128,192},{192,256},{256,320},{320,384},{384,448},... | collective-permute-start | bytes 294920 | tf_op jit(solution)/shard_map/ppermute | solution.py:25
  9.1 19.7 %collective-permute-start.1 = (f32[2,6,16,128]{3,2,1,0:T(8,128)S(1)}, f32[2,6,16,128]{3,2,1,0:T(8,128)S(1)}, u32[]{:S(2)}, u32[]{:S(2)}) collective-permute-start(f32[2,6,16,128]{3,2,1,0:T(8,128)S(1)} %get-tuple-element.1021), channel_id=1, source_target_pairs={{64,0},{128,64},{192,128},{256,192},{320,256},{384,320},{448,384},... | collective-permute-start | bytes 294920 | tf_op jit(solution)/shard_map/ppermute | solution.py:26
  15.1 81.4 %collective-permute-start.6 = (f32[8,8,64]{2,1,0:T(8,128)S(1)}, f32[8,8,64]{2,1,0:T(8,128)S(1)}, u32[]{:S(2)}, u32[]{:S(2)}) collective-permute-start(f32[8,8,64]{2,1,0:T(8,128)S(1)} %add_multiply_fusion.1), channel_id=1, source_target_pairs={{0,64},{64,128},{128,192},{192,256},{256,320},{320,384},{384,448},... | collective-permute-start | bytes 49160 | tf_op jit(solution)/shard_map/ppermute | solution.py:25
  19.7 45.4 %collective-permute-start.18 = (f32[1,4,32]{2,1,0:T(4,128)S(1)}, f32[1,4,32]{2,1,0:T(4,128)S(1)}, u32[]{:S(2)}, u32[]{:S(2)}) collective-permute-start(f32[1,4,32]{2,1,0:T(4,128)S(1)} %get-tuple-element.1069), channel_id=1, source_target_pairs={{0,64},{64,128},{128,192},{192,256},{256,320},{320,384},{384,448},... | collective-permute-start | bytes 1544 | tf_op jit(solution)/shard_map/ppermute | solution.py:119
  21.9 47.2 %collective-permute-start.19 = (f32[1,4,32]{2,1,0:T(4,128)S(1)}, f32[1,4,32]{2,1,0:T(4,128)S(1)}, u32[]{:S(2)}, u32[]{:S(2)}) collective-permute-start(f32[1,4,32]{2,1,0:T(4,128)S(1)} %get-tuple-element.1068), channel_id=1, source_target_pairs={{64,0},{128,64},{192,128},{256,192},{320,256},{384,320},{448,384},... | collective-permute-start | bytes 1544 | tf_op jit(solution)/shard_map/ppermute | solution.py:120
  25.3 14.8 %collective-permute-start.36 = (f32[1,2,16]{2,1,0:T(2,128)S(1)}, f32[1,2,16]{2,1,0:T(2,128)S(1)}, u32[]{:S(2)}, u32[]{:S(2)}) collective-permute-start(f32[1,2,16]{2,1,0:T(2,128)S(1)} %get-tuple-element.1107), channel_id=1, source_target_pairs={{0,64},{64,128},{128,192},{192,256},{256,320},{320,384},{384,448},... | collective-permute-start | bytes 392 | tf_op jit(solution)/shard_map/ppermute | solution.py:119
  53.7 42.8 %collective-permute-start.7 = (f32[8,8,64]{2,1,0:T(8,128)S(1)}, f32[8,8,64]{2,1,0:T(8,128)S(1)}, u32[]{:S(2)}, u32[]{:S(2)}) collective-permute-start(f32[8,8,64]{2,1,0:T(8,128)S(1)} %add_multiply_fusion.1), channel_id=1, source_target_pairs={{64,0},{128,64},{192,128},{256,192},{320,256},{384,320},{448,384},... | collective-permute-start | bytes 49160 | tf_op jit(solution)/shard_map/ppermute | solution.py:26
  58.0 18.4 %collective-permute-start.20 = (f32[4,1,32]{2,1,0:T(1,128)S(1)}, f32[4,1,32]{2,1,0:T(1,128)S(1)}, u32[]{:S(2)}, u32[]{:S(2)}) collective-permute-start(f32[4,1,32]{2,1,0:T(1,128)S(1)} %get-tuple-element.1067), channel_id=1, source_target_pairs={{0,4},{4,8},{8,12},{12,16},{16,20},{20,24},{24,28},{28,32},{32,36}... | collective-permute-start | bytes 1544 | tf_op jit(solution)/shard_map/ppermute | solution.py:119
  65.1 42.2 %collective-permute-start.2 = (f32[2,28,6,128]{3,0,2,1:T(2,128)S(1)}, f32[2,28,6,128]{3,0,2,1:T(2,128)S(1)}, u32[]{:S(2)}, u32[]{:S(2)}) collective-permute-start(f32[2,28,6,128]{3,0,2,1:T(2,128)S(1)} %copy.234), channel_id=1, source_target_pairs={{0,4},{4,8},{8,12},{12,16},{16,20},{20,24},{24,28},{28,32},{32,36}... | collective-permute-start | bytes 516104 | tf_op jit(solution)/shard_map/ppermute | solution.py:25
  69.2 38.2 %collective-permute-start.3 = (f32[2,28,6,128]{3,0,2,1:T(2,128)S(1)}, f32[2,28,6,128]{3,0,2,1:T(2,128)S(1)}, u32[]{:S(2)}, u32[]{:S(2)}) collective-permute-start(f32[2,28,6,128]{3,0,2,1:T(2,128)S(1)} %copy.235), channel_id=1, source_target_pairs={{4,0},{8,4},{12,8},{16,12},{20,16},{24,20},{28,24},{32,28},{36,32}... | collective-permute-start | bytes 516104 | tf_op jit(solution)/shard_map/ppermute | solution.py:26
  97.2 17.2 %collective-permute-start.8 = (f32[24,8,64]{2,1,0:T(8,128)}, f32[24,8,64]{2,1,0:T(8,128)}, u32[]{:S(2)}, u32[]{:S(2)}) collective-permute-start(f32[24,8,64]{2,1,0:T(8,128)} %pad_maximum_fusion.9), channel_id=1, source_target_pairs={{0,4},{4,8},{8,12},{12,16},{16,20},{20,24},{24,28},{28,32},{32,36}... | collective-permute-start | bytes 147464 | tf_op jit(solution)/shard_map/ppermute | solution.py:25
  99.9 14.5 %collective-permute-start.9 = (f32[24,8,64]{2,1,0:T(8,128)}, f32[24,8,64]{2,1,0:T(8,128)}, u32[]{:S(2)}, u32[]{:S(2)}) collective-permute-start(f32[24,8,64]{2,1,0:T(8,128)} %pad_maximum_fusion.9), channel_id=1, source_target_pairs={{4,0},{8,4},{12,8},{16,12},{20,16},{24,20},{28,24},{32,28},{36,32}... | collective-permute-start | bytes 147464 | tf_op jit(solution)/shard_map/ppermute | solution.py:26
  131.4 19.0 %collective-permute-start.12 = (f32[8,8,64]{2,1,0:T(8,128)S(1)}, f32[8,8,64]{2,1,0:T(8,128)S(1)}, u32[]{:S(2)}, u32[]{:S(2)}) collective-permute-start(f32[8,8,64]{2,1,0:T(8,128)S(1)} %add_multiply_fusion), channel_id=1, source_target_pairs={{0,64},{64,128},{128,192},{192,256},{256,320},{320,384},{384,448},... | collective-permute-start | bytes 49160 | tf_op jit(solution)/shard_map/ppermute | solution.py:25
  145.9 14.7 %collective-permute-start.10 = (f32[24,24,8]{2,1,0:T(8,128)S(1)}, f32[24,24,8]{2,1,0:T(8,128)S(1)}, u32[]{:S(2)}, u32[]{:S(2)}) collective-permute-start(f32[24,24,8]{2,1,0:T(8,128)S(1)} %get-tuple-element.1018), channel_id=1, source_target_pairs={{0,1},{1,2},{2,3},{4,5},{5,6},{6,7},{8,9},{9,10},{10,11},{12,13},{... | collective-permute-start | bytes 55304 | tf_op jit(solution)/shard_map/ppermute | solution.py:25
  152.3 15.6 %collective-permute-start.15 = (f32[24,8,64]{2,1,0:T(8,128)S(1)}, f32[24,8,64]{2,1,0:T(8,128)S(1)}, u32[]{:S(2)}, u32[]{:S(2)}) collective-permute-start(f32[24,8,64]{2,1,0:T(8,128)S(1)} %pad_maximum_fusion.10), channel_id=1, source_target_pairs={{4,0},{8,4},{12,8},{16,12},{20,16},{24,20},{28,24},{32,28},{36,32}... | collective-permute-start | bytes 147464 | tf_op jit(solution)/shard_map/ppermute | solution.py:26
  182.2 21.9 %collective-permute-start.24 = (f32[1,4,32]{2,1,0:T(4,128)S(1)}, f32[1,4,32]{2,1,0:T(4,128)S(1)}, u32[]{:S(2)}, u32[]{:S(2)}) collective-permute-start(f32[1,4,32]{2,1,0:T(4,128)S(1)} %get-tuple-element.1063), channel_id=1, source_target_pairs={{0,64},{64,128},{128,192},{192,256},{256,320},{320,384},{384,448},... | collective-permute-start | bytes 1544 | tf_op jit(solution)/shard_map/ppermute | solution.py:119
  190.2 16.0 %collective-permute-start.25 = (f32[1,4,32]{2,1,0:T(4,128)S(1)}, f32[1,4,32]{2,1,0:T(4,128)S(1)}, u32[]{:S(2)}, u32[]{:S(2)}) collective-permute-start(f32[1,4,32]{2,1,0:T(4,128)S(1)} %get-tuple-element.1062), channel_id=1, source_target_pairs={{64,0},{128,64},{192,128},{256,192},{320,256},{384,320},{448,384},... | collective-permute-start | bytes 1544 | tf_op jit(solution)/shard_map/ppermute | solution.py:120
  192.1 14.6 %collective-permute-start.26 = (f32[4,1,32]{2,1,0:T(1,128)S(1)}, f32[4,1,32]{2,1,0:T(1,128)S(1)}, u32[]{:S(2)}, u32[]{:S(2)}) collective-permute-start(f32[4,1,32]{2,1,0:T(1,128)S(1)} %get-tuple-element.1061), channel_id=1, source_target_pairs={{0,4},{4,8},{8,12},{12,16},{16,20},{20,24},{24,28},{28,32},{32,36}... | collective-permute-start | bytes 1544 | tf_op jit(solution)/shard_map/ppermute | solution.py:119
  209.4 20.8 %collective-permute-start.30 = (f32[1,4,32]{2,1,0:T(4,128)S(1)}, f32[1,4,32]{2,1,0:T(4,128)S(1)}, u32[]{:S(2)}, u32[]{:S(2)}) collective-permute-start(f32[1,4,32]{2,1,0:T(4,128)S(1)} %get-tuple-element.1057), channel_id=1, source_target_pairs={{0,64},{64,128},{128,192},{192,256},{256,320},{320,384},{384,448},... | collective-permute-start | bytes 1544 | tf_op jit(solution)/shard_map/ppermute | solution.py:119
  215.1 16.9 %collective-permute-start.31 = (f32[1,4,32]{2,1,0:T(4,128)S(1)}, f32[1,4,32]{2,1,0:T(4,128)S(1)}, u32[]{:S(2)}, u32[]{:S(2)}) collective-permute-start(f32[1,4,32]{2,1,0:T(4,128)S(1)} %get-tuple-element.1056), channel_id=1, source_target_pairs={{64,0},{128,64},{192,128},{256,192},{320,256},{384,320},{448,384},... | collective-permute-start | bytes 1544 | tf_op jit(solution)/shard_map/ppermute | solution.py:120
  217.0 15.5 %collective-permute-start.32 = (f32[4,1,32]{2,1,0:T(1,128)S(1)}, f32[4,1,32]{2,1,0:T(1,128)S(1)}, u32[]{:S(2)}, u32[]{:S(2)}) collective-permute-start(f32[4,1,32]{2,1,0:T(1,128)S(1)} %get-tuple-element.1055), channel_id=1, source_target_pairs={{0,4},{4,8},{8,12},{12,16},{16,20},{20,24},{24,28},{28,32},{32,36}... | collective-permute-start | bytes 1544 | tf_op jit(solution)/shard_map/ppermute | solution.py:119
  235.5 20.6 %collective-permute-start.42 = (f32[1,4,32]{2,1,0:T(4,128)S(1)}, f32[1,4,32]{2,1,0:T(4,128)S(1)}, u32[]{:S(2)}, u32[]{:S(2)}) collective-permute-start(f32[1,4,32]{2,1,0:T(4,128)S(1)} %get-tuple-element.1051), channel_id=1, source_target_pairs={{0,64},{64,128},{128,192},{192,256},{256,320},{320,384},{384,448},... | collective-permute-start | bytes 1544 | tf_op jit(solution)/shard_map/ppermute | solution.py:119
  241.2 16.7 %collective-permute-start.43 = (f32[1,4,32]{2,1,0:T(4,128)S(1)}, f32[1,4,32]{2,1,0:T(4,128)S(1)}, u32[]{:S(2)}, u32[]{:S(2)}) collective-permute-start(f32[1,4,32]{2,1,0:T(4,128)S(1)} %get-tuple-element.1050), channel_id=1, source_target_pairs={{64,0},{128,64},{192,128},{256,192},{320,256},{384,320},{448,384},... | collective-permute-start | bytes 1544 | tf_op jit(solution)/shard_map/ppermute | solution.py:120
  243.1 15.3 %collective-permute-start.44 = (f32[4,1,32]{2,1,0:T(1,128)S(1)}, f32[4,1,32]{2,1,0:T(1,128)S(1)}, u32[]{:S(2)}, u32[]{:S(2)}) collective-permute-start(f32[4,1,32]{2,1,0:T(1,128)S(1)} %get-tuple-element.1049), channel_id=1, source_target_pairs={{0,4},{4,8},{8,12},{12,16},{16,20},{20,24},{24,28},{28,32},{32,36}... | collective-permute-start | bytes 1544 | tf_op jit(solution)/shard_map/ppermute | solution.py:119
  261.8 20.5 %collective-permute-start.48 = (f32[1,2,16]{2,1,0:T(2,128)S(1)}, f32[1,2,16]{2,1,0:T(2,128)S(1)}, u32[]{:S(2)}, u32[]{:S(2)}) collective-permute-start(f32[1,2,16]{2,1,0:T(2,128)S(1)} %get-tuple-element.1101), channel_id=1, source_target_pairs={{0,64},{64,128},{128,192},{192,256},{256,320},{320,384},{384,448},... | collective-permute-start | bytes 392 | tf_op jit(solution)/shard_map/ppermute | solution.py:119
  267.5 16.8 %collective-permute-start.49 = (f32[1,2,16]{2,1,0:T(2,128)S(1)}, f32[1,2,16]{2,1,0:T(2,128)S(1)}, u32[]{:S(2)}, u32[]{:S(2)}) collective-permute-start(f32[1,2,16]{2,1,0:T(2,128)S(1)} %get-tuple-element.1100), channel_id=1, source_target_pairs={{64,0},{128,64},{192,128},{256,192},{320,256},{384,320},{448,384},... | collective-permute-start | bytes 392 | tf_op jit(solution)/shard_map/ppermute | solution.py:120
  269.4 15.4 %collective-permute-start.50 = (f32[2,1,16]{2,1,0:T(1,128)S(1)}, f32[2,1,16]{2,1,0:T(1,128)S(1)}, u32[]{:S(2)}, u32[]{:S(2)}) collective-permute-start(f32[2,1,16]{2,1,0:T(1,128)S(1)} %get-tuple-element.1099), channel_id=1, source_target_pairs={{0,4},{4,8},{8,12},{12,16},{16,20},{20,24},{24,28},{28,32},{32,36}... | collective-permute-start | bytes 392 | tf_op jit(solution)/shard_map/ppermute | solution.py:119
  287.3 20.0 %collective-permute-start.54 = (f32[1,2,16]{2,1,0:T(2,128)S(1)}, f32[1,2,16]{2,1,0:T(2,128)S(1)}, u32[]{:S(2)}, u32[]{:S(2)}) collective-permute-start(f32[1,2,16]{2,1,0:T(2,128)S(1)} %get-tuple-element.1095), channel_id=1, source_target_pairs={{0,64},{64,128},{128,192},{192,256},{256,320},{320,384},{384,448},... | collective-permute-start | bytes 392 | tf_op jit(solution)/shard_map/ppermute | solution.py:119
  293.0 16.2 %collective-permute-start.55 = (f32[1,2,16]{2,1,0:T(2,128)S(1)}, f32[1,2,16]{2,1,0:T(2,128)S(1)}, u32[]{:S(2)}, u32[]{:S(2)}) collective-permute-start(f32[1,2,16]{2,1,0:T(2,128)S(1)} %get-tuple-element.1094), channel_id=1, source_target_pairs={{64,0},{128,64},{192,128},{256,192},{320,256},{384,320},{448,384},... | collective-permute-start | bytes 392 | tf_op jit(solution)/shard_map/ppermute | solution.py:120
  294.9 14.9 %collective-permute-start.56 = (f32[2,1,16]{2,1,0:T(1,128)S(1)}, f32[2,1,16]{2,1,0:T(1,128)S(1)}, u32[]{:S(2)}, u32[]{:S(2)}) collective-permute-start(f32[2,1,16]{2,1,0:T(1,128)S(1)} %get-tuple-element.1093), channel_id=1, source_target_pairs={{0,4},{4,8},{8,12},{12,16},{16,20},{20,24},{24,28},{28,32},{32,36}... | collective-permute-start | bytes 392 | tf_op jit(solution)/shard_map/ppermute | solution.py:119
  312.3 20.0 %collective-permute-start.60 = (f32[1,2,16]{2,1,0:T(2,128)S(1)}, f32[1,2,16]{2,1,0:T(2,128)S(1)}, u32[]{:S(2)}, u32[]{:S(2)}) collective-permute-start(f32[1,2,16]{2,1,0:T(2,128)S(1)} %get-tuple-element.1089), channel_id=1, source_target_pairs={{0,64},{64,128},{128,192},{192,256},{256,320},{320,384},{384,448},... | collective-permute-start | bytes 392 | tf_op jit(solution)/shard_map/ppermute | solution.py:119
  317.9 16.2 %collective-permute-start.61 = (f32[1,2,16]{2,1,0:T(2,128)S(1)}, f32[1,2,16]{2,1,0:T(2,128)S(1)}, u32[]{:S(2)}, u32[]{:S(2)}) collective-permute-start(f32[1,2,16]{2,1,0:T(2,128)S(1)} %get-tuple-element.1088), channel_id=1, source_target_pairs={{64,0},{128,64},{192,128},{256,192},{320,256},{384,320},{448,384},... | collective-permute-start | bytes 392 | tf_op jit(solution)/shard_map/ppermute | solution.py:120
  319.8 14.9 %collective-permute-start.62 = (f32[2,1,16]{2,1,0:T(1,128)S(1)}, f32[2,1,16]{2,1,0:T(1,128)S(1)}, u32[]{:S(2)}, u32[]{:S(2)}) collective-permute-start(f32[2,1,16]{2,1,0:T(1,128)S(1)} %get-tuple-element.1087), channel_id=1, source_target_pairs={{0,4},{4,8},{8,12},{12,16},{16,20},{20,24},{24,28},{28,32},{32,36}... | collective-permute-start | bytes 392 | tf_op jit(solution)/shard_map/ppermute | solution.py:119
  337.2 20.0 %collective-permute-start.66 = (f32[1,2,16]{2,1,0:T(2,128)S(1)}, f32[1,2,16]{2,1,0:T(2,128)S(1)}, u32[]{:S(2)}, u32[]{:S(2)}) collective-permute-start(f32[1,2,16]{2,1,0:T(2,128)S(1)} %get-tuple-element.1083), channel_id=1, source_target_pairs={{0,64},{64,128},{128,192},{192,256},{256,320},{320,384},{384,448},... | collective-permute-start | bytes 392 | tf_op jit(solution)/shard_map/ppermute | solution.py:119
  342.8 16.6 %collective-permute-start.67 = (f32[1,2,16]{2,1,0:T(2,128)S(1)}, f32[1,2,16]{2,1,0:T(2,128)S(1)}, u32[]{:S(2)}, u32[]{:S(2)}) collective-permute-start(f32[1,2,16]{2,1,0:T(2,128)S(1)} %get-tuple-element.1082), channel_id=1, source_target_pairs={{64,0},{128,64},{192,128},{256,192},{320,256},{384,320},{448,384},... | collective-permute-start | bytes 392 | tf_op jit(solution)/shard_map/ppermute | solution.py:120
  344.8 15.3 %collective-permute-start.68 = (f32[2,1,16]{2,1,0:T(1,128)S(1)}, f32[2,1,16]{2,1,0:T(1,128)S(1)}, u32[]{:S(2)}, u32[]{:S(2)}) collective-permute-start(f32[2,1,16]{2,1,0:T(1,128)S(1)} %get-tuple-element.1081), channel_id=1, source_target_pairs={{0,4},{4,8},{8,12},{12,16},{16,20},{20,24},{24,28},{28,32},{32,36}... | collective-permute-start | bytes 392 | tf_op jit(solution)/shard_map/ppermute | solution.py:119
  362.2 20.4 %collective-permute-start.72 = (f32[1,2,16]{2,1,0:T(2,128)S(1)}, f32[1,2,16]{2,1,0:T(2,128)S(1)}, u32[]{:S(2)}, u32[]{:S(2)}) collective-permute-start(f32[1,2,16]{2,1,0:T(2,128)S(1)} %get-tuple-element.1077), channel_id=1, source_target_pairs={{0,64},{64,128},{128,192},{192,256},{256,320},{320,384},{384,448},... | collective-permute-start | bytes 392 | tf_op jit(solution)/shard_map/ppermute | solution.py:119
  367.8 16.6 %collective-permute-start.73 = (f32[1,2,16]{2,1,0:T(2,128)S(1)}, f32[1,2,16]{2,1,0:T(2,128)S(1)}, u32[]{:S(2)}, u32[]{:S(2)}) collective-permute-start(f32[1,2,16]{2,1,0:T(2,128)S(1)} %get-tuple-element.1076), channel_id=1, source_target_pairs={{64,0},{128,64},{192,128},{256,192},{320,256},{384,320},{448,384},... | collective-permute-start | bytes 392 | tf_op jit(solution)/shard_map/ppermute | solution.py:120
  369.7 15.3 %collective-permute-start.74 = (f32[2,1,16]{2,1,0:T(1,128)S(1)}, f32[2,1,16]{2,1,0:T(1,128)S(1)}, u32[]{:S(2)}, u32[]{:S(2)}) collective-permute-start(f32[2,1,16]{2,1,0:T(1,128)S(1)} %get-tuple-element.1075), channel_id=1, source_target_pairs={{0,4},{4,8},{8,12},{12,16},{16,20},{20,24},{24,28},{28,32},{32,36}... | collective-permute-start | bytes 392 | tf_op jit(solution)/shard_map/ppermute | solution.py:119
  387.7 20.1 %collective-permute-start.78 = (f32[1,4,32]{2,1,0:T(4,128)S(1)}, f32[1,4,32]{2,1,0:T(4,128)S(1)}, u32[]{:S(2)}, u32[]{:S(2)}) collective-permute-start(f32[1,4,32]{2,1,0:T(4,128)S(1)} %get-tuple-element.1045), channel_id=1, source_target_pairs={{0,64},{64,128},{128,192},{192,256},{256,320},{320,384},{384,448},... | collective-permute-start | bytes 1544 | tf_op jit(solution)/shard_map/ppermute | solution.py:119
  393.4 16.2 %collective-permute-start.79 = (f32[1,4,32]{2,1,0:T(4,128)S(1)}, f32[1,4,32]{2,1,0:T(4,128)S(1)}, u32[]{:S(2)}, u32[]{:S(2)}) collective-permute-start(f32[1,4,32]{2,1,0:T(4,128)S(1)} %get-tuple-element.1044), channel_id=1, source_target_pairs={{64,0},{128,64},{192,128},{256,192},{320,256},{384,320},{448,384},... | collective-permute-start | bytes 1544 | tf_op jit(solution)/shard_map/ppermute | solution.py:120
  395.3 14.7 %collective-permute-start.80 = (f32[4,1,32]{2,1,0:T(1,128)S(1)}, f32[4,1,32]{2,1,0:T(1,128)S(1)}, u32[]{:S(2)}, u32[]{:S(2)}) collective-permute-start(f32[4,1,32]{2,1,0:T(1,128)S(1)} %get-tuple-element.1043), channel_id=1, source_target_pairs={{0,4},{4,8},{8,12},{12,16},{16,20},{20,24},{24,28},{28,32},{32,36}... | collective-permute-start | bytes 1544 | tf_op jit(solution)/shard_map/ppermute | solution.py:119
  413.0 20.6 %collective-permute-start.84 = (f32[1,4,32]{2,1,0:T(4,128)S(1)}, f32[1,4,32]{2,1,0:T(4,128)S(1)}, u32[]{:S(2)}, u32[]{:S(2)}) collective-permute-start(f32[1,4,32]{2,1,0:T(4,128)S(1)} %get-tuple-element.1039), channel_id=1, source_target_pairs={{0,64},{64,128},{128,192},{192,256},{256,320},{320,384},{384,448},... | collective-permute-start | bytes 1544 | tf_op jit(solution)/shard_map/ppermute | solution.py:119
  418.7 16.7 %collective-permute-start.85 = (f32[1,4,32]{2,1,0:T(4,128)S(1)}, f32[1,4,32]{2,1,0:T(4,128)S(1)}, u32[]{:S(2)}, u32[]{:S(2)}) collective-permute-start(f32[1,4,32]{2,1,0:T(4,128)S(1)} %get-tuple-element.1038), channel_id=1, source_target_pairs={{64,0},{128,64},{192,128},{256,192},{320,256},{384,320},{448,384},... | collective-permute-start | bytes 1544 | tf_op jit(solution)/shard_map/ppermute | solution.py:120
  420.7 15.3 %collective-permute-start.86 = (f32[4,1,32]{2,1,0:T(1,128)S(1)}, f32[4,1,32]{2,1,0:T(1,128)S(1)}, u32[]{:S(2)}, u32[]{:S(2)}) collective-permute-start(f32[4,1,32]{2,1,0:T(1,128)S(1)} %get-tuple-element.1037), channel_id=1, source_target_pairs={{0,4},{4,8},{8,12},{12,16},{16,20},{20,24},{24,28},{28,32},{32,36}... | collective-permute-start | bytes 1544 | tf_op jit(solution)/shard_map/ppermute | solution.py:119
  438.9 20.6 %collective-permute-start.90 = (f32[1,4,32]{2,1,0:T(4,128)S(1)}, f32[1,4,32]{2,1,0:T(4,128)S(1)}, u32[]{:S(2)}, u32[]{:S(2)}) collective-permute-start(f32[1,4,32]{2,1,0:T(4,128)S(1)} %get-tuple-element.1033), channel_id=1, source_target_pairs={{0,64},{64,128},{128,192},{192,256},{256,320},{320,384},{384,448},... | collective-permute-start | bytes 1544 | tf_op jit(solution)/shard_map/ppermute | solution.py:119
  444.6 16.7 %collective-permute-start.91 = (f32[1,4,32]{2,1,0:T(4,128)S(1)}, f32[1,4,32]{2,1,0:T(4,128)S(1)}, u32[]{:S(2)}, u32[]{:S(2)}) collective-permute-start(f32[1,4,32]{2,1,0:T(4,128)S(1)} %get-tuple-element.1032), channel_id=1, source_target_pairs={{64,0},{128,64},{192,128},{256,192},{320,256},{384,320},{448,384},... | collective-permute-start | bytes 1544 | tf_op jit(solution)/shard_map/ppermute | solution.py:120
  446.5 15.3 %collective-permute-start.92 = (f32[4,1,32]{2,1,0:T(1,128)S(1)}, f32[4,1,32]{2,1,0:T(1,128)S(1)}, u32[]{:S(2)}, u32[]{:S(2)}) collective-permute-start(f32[4,1,32]{2,1,0:T(1,128)S(1)} %get-tuple-element.1031), channel_id=1, source_target_pairs={{0,4},{4,8},{8,12},{12,16},{16,20},{20,24},{24,28},{28,32},{32,36}... | collective-permute-start | bytes 1544 | tf_op jit(solution)/shard_map/ppermute | solution.py:119
  (98 other events, 891.5 us)
